TPU v7x, 256 devices: a whole 4x4x8 slice. The times are simulated.
256 devices in a mesh: src: 16 (over y, x), tgt: 16 (over z, core).
Axes of the slice: x: 4, y: 4, z: 8, core: 2. Of those that a mesh axis runs over, the one named last changes fastest.
Arguments:
- src_emb_t: bfloat16 [300, 16384], P(None, 'src'), may hold values from -6 to 6
- tgt_emb_t: bfloat16 [300, 32768], P(None, 'tgt'), may hold values from -6 to 6
- core: float32 [300, 300], replicated, may hold values from -0.08 to 0.2
- src_logw: float32 [16384], P('src'), may hold values from -1.5 to 1.5
- tgt_logw: float32 [32768], P('tgt'), may hold values from -1.5 to 1.5
Outputs:
- src_potential: float32 [16384], P('src')
- tgt_potential: float32 [32768], P('tgt')
- next_core: float32 [300, 300], replicated
All inputs are finite; a program needn't handle non-finite values.
Results may differ from a plain program's by a relative error of at most 0.0036.
Values sent between devices are 32-bit elements; how exact they have to be, the bound alone decides.
No kernel may reach another device: no remote copies, remote signals or barrier semaphores. Data moves between devices by JAX's collectives and lax.ppermute only.
A program may use at most 64 MiB of HBM per device.

v0:
```python
import jax
import jax.numpy as jnp
from jax import lax
from jax.sharding import PartitionSpec as P

D = 300
ITERS = 3


def row_lse(shifted):
    peaks = jnp.max(shifted, axis=1)
    peaks = lax.pmax(peaks, "tgt")
    totals = lax.psum(jnp.sum(jnp.exp(shifted - peaks[:, None]), axis=1), "tgt")
    return peaks + jnp.log(totals)


def col_lse(shifted):
    peaks = jnp.max(shifted, axis=0)
    peaks = lax.pmax(peaks, "src")
    totals = lax.psum(jnp.sum(jnp.exp(shifted - peaks[None, :]), axis=0), "src")
    return peaks + jnp.log(totals)


def per_device(src_emb_t, tgt_emb_t, core, src_logw, tgt_logw):
    projected = jnp.dot(
        core.T, src_emb_t.astype(jnp.float32), precision=lax.Precision.HIGHEST
    ).astype(jnp.bfloat16)

    def scores_of():
        return lax.dot_general(
            projected, tgt_emb_t, (((0,), (0,)), ((), ())), preferred_element_type=jnp.float32
        )

    stored = scores_of()
    tgt_pot = jnp.zeros((tgt_emb_t.shape[1],), jnp.float32)
    src_pot = jnp.zeros((src_emb_t.shape[1],), jnp.float32)
    for step in range(ITERS):
        current = stored if step == 0 else scores_of()
        src_pot = src_logw - row_lse(current + tgt_pot[None, :])
        current = scores_of()
        tgt_pot = tgt_logw - col_lse(current + src_pot[:, None])
    current = scores_of()
    plan = jnp.exp(current + src_pot[:, None] + tgt_pot[None, :]).astype(jnp.bfloat16)
    total_words = src_emb_t.shape[1] * lax.axis_size("src")
    share = src_emb_t.shape[1] // lax.axis_size("tgt")
    portion = lax.psum_scatter(
        lax.dot_general(
            plan, tgt_emb_t, (((1,), (1,)), ((), ())), preferred_element_type=jnp.float32
        ),
        "tgt",
        scatter_dimension=0,
        tiled=True,
    )
    offset = lax.axis_index("tgt") * share
    my_words = lax.dynamic_slice_in_dim(src_emb_t, offset, share, 1)
    partial_core = jnp.dot(my_words.astype(jnp.float32), portion, precision=lax.Precision.HIGHEST)
    summed = lax.psum(partial_core, ("src", "tgt"))
    next_core = summed * (D / total_words)
    return (src_pot, tgt_pot, next_core)


def solution(mesh):
    placed = (P(None, "src"), P(None, "tgt"), P(), P("src"), P("tgt"))
    return jax.shard_map(
        per_device, mesh=mesh, in_specs=placed, out_specs=(P("src"), P("tgt"), P()), check_vma=False
    )
```

profile of v0, /device:TPU:1, one launch (start us, length us, event | category | flops | bytes accessed | tf_op | source)
XLA Modules:
  0.0 761.1 jit_solution(15984662700582594350)
XLA Ops:
  7.2 0.0 copy-start
  7.2 0.0 reduce-scatter.2.cloned.1.call-start
  7.2 2.5 convolution_convert_fusion
  9.7 0.0 copy-done
  9.7 0.0 copy-start.3
  9.7 5.6 fusion.6
  15.4 27.4 %pmax.42 = f32[1024]{0:T(1024)S(1)} all-reduce(f32[1024]{0:T(1024)S(1)} %get-tuple-element.3), channel_id=1, replica_groups=mesh['src'=16,'tgt'=16] {'tgt'}, use_global_device_ids=true, to_apply=%region_1.0 | all-reduce | flops 1024 | bytes 8192 | tf_op jit(solution)/shard_map/pmax | solution.py:12
  42.8 4.6 exponential_reduce_fusion.5
  47.4 25.8 %psum.49 = f32[1024]{0:T(1024)S(1)} all-reduce(f32[1024]{0:T(1024)S(1)} %exponential_reduce_fusion.5), channel_id=1, replica_groups=mesh['src'=16,'tgt'=16] {'tgt'}, use_global_device_ids=true, to_apply=%region_3.0 | all-reduce | flops 1024 | bytes 8192 | tf_op jit(solution)/shard_map/psum | solution.py:13
  73.2 0.0 copy-done.3
  73.2 0.0 copy-start.1
  73.2 4.0 add_reduce_fusion.3
  77.2 33.9 %pmax.43 = f32[2048]{0:T(1024)S(1)} all-reduce(f32[2048]{0:T(1024)S(1)} %add_reduce_fusion.3), channel_id=1, replica_groups=mesh['src'=16,'tgt'=16] {'src'}, use_global_device_ids=true, to_apply=%region_5.0 | all-reduce | flops 2048 | bytes 16384 | tf_op jit(solution)/shard_map/pmax | solution.py:19
  111.2 4.3 exponential_reduce_fusion.4
  115.5 29.0 %psum.50 = f32[2048]{0:T(1024)S(1)} all-reduce(f32[2048]{0:T(1024)S(1)} %exponential_reduce_fusion.4), channel_id=1, replica_groups=mesh['src'=16,'tgt'=16] {'src'}, use_global_device_ids=true, to_apply=%region_7.0 | all-reduce | flops 2048 | bytes 16384 | tf_op jit(solution)/shard_map/psum | solution.py:20
  144.5 0.0 copy-done.1
  144.5 4.0 add_reduce_fusion.2
  148.6 37.7 %pmax.44 = f32[1024]{0:T(1024)S(1)} all-reduce(f32[1024]{0:T(1024)S(1)} %add_reduce_fusion.2), channel_id=1, replica_groups=mesh['src'=16,'tgt'=16] {'tgt'}, use_global_device_ids=true, to_apply=%region_9.0 | all-reduce | flops 1024 | bytes 8192 | tf_op jit(solution)/shard_map/pmax | solution.py:12
  186.3 4.4 exponential_reduce_fusion.3
  190.7 23.6 %psum.51 = f32[1024]{0:T(1024)S(1)} all-reduce(f32[1024]{0:T(1024)S(1)} %exponential_reduce_fusion.3), channel_id=1, replica_groups=mesh['src'=16,'tgt'=16] {'tgt'}, use_global_device_ids=true, to_apply=%region_11.0 | all-reduce | flops 1024 | bytes 8192 | tf_op jit(solution)/shard_map/psum | solution.py:13
  214.2 4.0 add_reduce_fusion.1
  218.3 31.0 %pmax.45 = f32[2048]{0:T(1024)S(1)} all-reduce(f32[2048]{0:T(1024)S(1)} %add_reduce_fusion.1), channel_id=1, replica_groups=mesh['src'=16,'tgt'=16] {'src'}, use_global_device_ids=true, to_apply=%region_13.0 | all-reduce | flops 2048 | bytes 16384 | tf_op jit(solution)/shard_map/pmax | solution.py:19
  249.3 4.3 exponential_reduce_fusion.2
  253.6 29.0 %psum.52 = f32[2048]{0:T(1024)S(1)} all-reduce(f32[2048]{0:T(1024)S(1)} %exponential_reduce_fusion.2), channel_id=1, replica_groups=mesh['src'=16,'tgt'=16] {'src'}, use_global_device_ids=true, to_apply=%region_15.0 | all-reduce | flops 2048 | bytes 16384 | tf_op jit(solution)/shard_map/psum | solution.py:20
  282.7 4.0 add_reduce_fusion
  286.7 37.6 %pmax.46 = f32[1024]{0:T(1024)S(1)} all-reduce(f32[1024]{0:T(1024)S(1)} %add_reduce_fusion), channel_id=1, replica_groups=mesh['src'=16,'tgt'=16] {'tgt'}, use_global_device_ids=true, to_apply=%region_17.0 | all-reduce | flops 1024 | bytes 8192 | tf_op jit(solution)/shard_map/pmax | solution.py:12
  324.3 4.4 exponential_reduce_fusion.1
  328.7 23.6 %psum.53 = f32[1024]{0:T(1024)S(1)} all-reduce(f32[1024]{0:T(1024)S(1)} %exponential_reduce_fusion.1), channel_id=1, replica_groups=mesh['src'=16,'tgt'=16] {'tgt'}, use_global_device_ids=true, to_apply=%region_19.0 | all-reduce | flops 1024 | bytes 8192 | tf_op jit(solution)/shard_map/psum | solution.py:13
  352.3 0.0 copy-start.2
  352.3 4.0 add_reduce_fusion.4
  356.3 30.7 %pmax.47 = f32[2048]{0:T(1024)S(1)} all-reduce(f32[2048]{0:T(1024)S(1)} %add_reduce_fusion.4), channel_id=1, replica_groups=mesh['src'=16,'tgt'=16] {'src'}, use_global_device_ids=true, to_apply=%region_21.0 | all-reduce | flops 2048 | bytes 16384 | tf_op jit(solution)/shard_map/pmax | solution.py:19
  387.0 4.3 exponential_reduce_fusion
  391.3 29.0 %psum.54 = f32[2048]{0:T(1024)S(1)} all-reduce(f32[2048]{0:T(1024)S(1)} %exponential_reduce_fusion), channel_id=1, replica_groups=mesh['src'=16,'tgt'=16] {'src'}, use_global_device_ids=true, to_apply=%region_23.0 | all-reduce | flops 2048 | bytes 16384 | tf_op jit(solution)/shard_map/psum | solution.py:20
  420.3 0.0 copy-done.2
  420.4 0.0 copy-start.4
  420.4 7.0 fusion
  427.4 0.0 copy-done.4
  427.4 0.0 reduce-scatter.2.cloned.1.call-update
  427.4 0.0 all-reduce.2.cloned.1.call-start
  427.5 64.5 %reduce-scatter.2.cloned.1.call-done = f32[64,300]{1,0:T(8,128)} async-done(((f32[1024,300]{1,0:T(8,128)}), f32[64,300]{1,0:T(8,128)}) %reduce-scatter.2.cloned.1.call-update) | async-done | bytes 76816 | tf_op jit(solution)/shard_map/reduce_scatter | solution.py:46
  492.0 2.1 fusion.3
  494.1 0.0 all-reduce.2.cloned.1.call-update
  494.1 258.3 %all-reduce.2.cloned.1.call-done = f32[300,300]{1,0:T(8,128)} async-done(((f32[300,300]{1,0:T(8,128)}), f32[300,300]{1,0:T(8,128)}) %all-reduce.2.cloned.1.call-update) | async-done | bytes 360016 | tf_op jit(solution)/shard_map/psum | solution.py:57
  752.4 1.8 broadcast_multiply_fusion
  (6 shorter events, 0.1 us)
Async XLA Ops:
  7.2 2.6 copy-start
  7.2 484.8 %reduce-scatter.2.cloned.1.call-start = ((), (), s32[]{:S(2)}) async-start(), calls=%async_computation.1 | async-start | bytes 1671168 | tf_op jit(solution)/shard_map/reduce_scatter | solution.py:46
  9.7 63.5 %copy-start.3 = (f32[1024]{0:T(1024)S(1)}, f32[1024]{0:T(1024)}, u32[]{:S(2)}) copy-start(f32[1024]{0:T(1024)} %param.8) | copy-start | bytes 12292
  73.2 71.3 %copy-start.1 = (f32[2048]{0:T(1024)S(1)}, f32[2048]{0:T(1024)}, u32[]{:S(2)}) copy-start(f32[2048]{0:T(1024)} %param.9) | copy-start | bytes 24580
  352.3 68.1 %copy-start.2 = (f32[1024]{0:T(1024)}, f32[1024]{0:T(1024)S(1)}, u32[]{:S(2)}) copy-start(f32[1024]{0:T(1024)S(1)} %add_subtract_fusion.3) | copy-start | bytes 12292
  420.4 7.0 copy-start.4
  427.4 325.0 %all-reduce.2.cloned.1.call-start = ((), (), s32[]{:S(2)}) async-start(), calls=%async_computation.2 | async-start | bytes 933888 | tf_op jit(solution)/shard_map/psum | solution.py:57
Sparse Core Ops, SparseCore 0:
  427.5 64.4 reduce-scatter.1
  498.1 254.2 all-reduce.1
where the time goes:
time: 763 us; the launch traced here: 761 us
  blocking collectives  358 us (47%)
  waiting for transfers between devices  323 us (42%)
  other arithmetic  48.2 us (6%)
  matrix products  17.2 us (2%)
  between operations  14.3 us (2%)
    psum x1, waiting for transfers between devices, per_device(): summed = lax.psum(partial_core, ('src', 'tgt'))  258 us
    pmax x3, blocking collectives, row_lse(): peaks = lax.pmax(peaks, 'tgt')  103 us
    pmax x3, blocking collectives, col_lse(): peaks = lax.pmax(peaks, 'src')  95.7 us
    psum x3, blocking collectives, col_lse(): totals = lax.psum(jnp.sum(jnp.exp(shifted - peaks[None, :]), axis=0), 'src')  87 us
    psum x3, blocking collectives, row_lse(): totals = lax.psum(jnp.sum(jnp.exp(shifted - peaks[:, None]), axis=1), 'tgt')  72.9 us
    reduce_scatter x1, waiting for transfers between devices, per_device(): lax.psum_scatter(lax.dot_general(plan, tgt_emb_t, (((1,), (1,)), ((), ())...  64.5 us
  transfers between devices with their start and end apart: 2, of which 2 were waited for; matrix products, arithmetic and copies ran while one was open for 0% of the time, Pallas kernels for 0%

commit v1 on v0

v1 whole, which is shorter than its diff:
```python
import jax
import jax.numpy as jnp
from jax import lax
from jax.sharding import PartitionSpec as P

D = 300
ITERS = 3


def merge_lse(peaks, totals, axis):
    n = lax.axis_size(axis)
    pair = jnp.stack([peaks, totals])
    sent = jnp.broadcast_to(pair[None], (n,) + pair.shape)
    got = lax.all_to_all(sent, axis, 0, 0, tiled=False)
    top = jnp.max(got[:, 0], axis=0)
    total = jnp.sum(got[:, 1] * jnp.exp(got[:, 0] - top[None]), axis=0)
    return top + jnp.log(total)


def row_lse(shifted):
    peaks = jnp.max(shifted, axis=1)
    totals = jnp.sum(jnp.exp(shifted - peaks[:, None]), axis=1)
    return merge_lse(peaks, totals, "tgt")


def col_lse(shifted):
    peaks = jnp.max(shifted, axis=0)
    totals = jnp.sum(jnp.exp(shifted - peaks[None, :]), axis=0)
    return merge_lse(peaks, totals, "src")


def butterfly_sum(x, axis):
    n = lax.axis_size(axis)
    d = 1
    while d < n:
        x = x + lax.ppermute(x, axis, [(i, i ^ d) for i in range(n)])
        d *= 2
    return x


def sum_all(c):
    n = lax.axis_size("tgt")
    rows = c.shape[0]
    padded = -(-rows // n) * n
    x = jnp.pad(c, ((0, padded - rows), (0, 0)))
    idx = lax.axis_index("tgt")
    d = n // 2
    while d >= 1:
        half = x.shape[0] // 2
        lo, hi = x[:half], x[half:]
        upper = (idx // d) % 2 == 1
        send = jnp.where(upper, lo, hi)
        keep = jnp.where(upper, hi, lo)
        x = keep + lax.ppermute(send, "tgt", [(i, i ^ d) for i in range(n)])
        d //= 2
    x = butterfly_sum(x, "src")
    d = 1
    while d < n:
        upper = (idx // d) % 2 == 1
        other = lax.ppermute(x, "tgt", [(i, i ^ d) for i in range(n)])
        x = jnp.where(upper, jnp.concatenate([other, x]), jnp.concatenate([x, other]))
        d *= 2
    return x[:rows]


def per_device(src_emb_t, tgt_emb_t, core, src_logw, tgt_logw):
    projected = jnp.dot(
        core.T, src_emb_t.astype(jnp.float32), precision=lax.Precision.HIGHEST
    ).astype(jnp.bfloat16)
    scores = lax.dot_general(
        projected, tgt_emb_t, (((0,), (0,)), ((), ())), preferred_element_type=jnp.float32
    )
    tgt_pot = jnp.zeros((tgt_emb_t.shape[1],), jnp.float32)
    src_pot = jnp.zeros((src_emb_t.shape[1],), jnp.float32)
    for step in range(ITERS):
        src_pot = src_logw - row_lse(scores + tgt_pot[None, :])
        tgt_pot = tgt_logw - col_lse(scores + src_pot[:, None])
    plan = jnp.exp(scores + src_pot[:, None] + tgt_pot[None, :]).astype(jnp.bfloat16)
    total_words = src_emb_t.shape[1] * lax.axis_size("src")
    panel = lax.dot_general(
        plan, tgt_emb_t, (((1,), (1,)), ((), ())), preferred_element_type=jnp.float32
    )
    partial_core = jnp.dot(src_emb_t.astype(jnp.float32), panel, precision=lax.Precision.HIGHEST)
    next_core = sum_all(partial_core) * (D / total_words)
    return (src_pot, tgt_pot, next_core)


def solution(mesh):
    placed = (P(None, "src"), P(None, "tgt"), P(), P("src"), P("tgt"))
    return jax.shard_map(
        per_device, mesh=mesh, in_specs=placed, out_specs=(P("src"), P("tgt"), P()), check_vma=False
    )
```

time: 763 us -> 186 us (0.24)
  blocking collectives: 358 us -> 70.3 us
  waiting for transfers between devices: 323 us -> 71 us
  other arithmetic: 48.2 us -> 16.4 us
  starting transfers between devices: 0.08 us -> 14.4 us
  between operations: 14.3 us -> 1.2 us
    psum x1 -> x0, waiting for transfers between devices: 258 us -> none  [per_device(): summed = lax.psum(partial_core, ('src', 'tgt'))]
    pmax x6 -> x0, blocking collectives: 198 us -> none  [the longest x3 103 us: row_lse(): peaks = lax.pmax(peaks, 'tgt')]
    psum x6 -> x0, blocking collectives: 160 us -> none  [the longest x3 87 us: col_lse(): totals = lax.psum(jnp.sum(jnp.exp(shifted - peaks[None, :]), axis=0), 'src')]
    all_to_all x0 -> x5, blocking collectives: none -> 70.3 us  [merge_lse(): got = lax.all_to_all(sent, axis, 0, 0, tiled=False)]
    reduce_scatter x1 -> x0, waiting for transfers between devices: 64.5 us -> none  [per_device(): lax.psum_scatter(lax.dot_general(plan, tgt_emb_t, (((1,), (1,)), ((), ())...]
    ppermute x0 -> x12, waiting for transfers between devices: none -> 61.9 us  [the longest x4 24.9 us: sum_all(): x = keep + lax.ppermute(send, 'tgt', [(i, i ^ d) for i in range(n)])]
    reduce_sum x6 -> x12, other arithmetic: 26.3 us -> 11 us  [the longest x3 5.44 us: col_lse(): totals = jnp.sum(jnp.exp(shifted - peaks[None, :]), axis=0)]
    ppermute x0 -> x12, starting transfers between devices: none -> 10.9 us  [the longest x4 6.07 us: sum_all(): other = lax.ppermute(x, 'tgt', [(i, i ^ d) for i in range(n)])]
  transfers between devices with their start and end apart: 2 -> 13, of which waited for: 2 -> 13; matrix products, arithmetic and copies ran while one was open for 0% -> 0% of each run, Pallas kernels for 0% -> 0%
where the time goes in v1:
time: 186 us
  waiting for transfers between devices  71 us (38%)
  blocking collectives  70.3 us (38%)
  other arithmetic  16.4 us (9%)
  starting transfers between devices  14.4 us (8%)
  matrix products  11.2 us (6%)
    all_to_all x5, blocking collectives, merge_lse(): got = lax.all_to_all(sent, axis, 0, 0, tiled=False)  70.3 us
    ppermute x4, waiting for transfers between devices, sum_all(): x = keep + lax.ppermute(send, 'tgt', [(i, i ^ d) for i in range(n)])  24.9 us
    ppermute x4, waiting for transfers between devices, sum_all(): other = lax.ppermute(x, 'tgt', [(i, i ^ d) for i in range(n)])  24.5 us
    ppermute x4, waiting for transfers between devices, butterfly_sum(): x = x + lax.ppermute(x, axis, [(i, i ^ d) for i in range(n)])  12.5 us
    all_to_all x1, waiting for transfers between devices, merge_lse(): got = lax.all_to_all(sent, axis, 0, 0, tiled=False)  9.07 us
    ppermute x4, starting transfers between devices, sum_all(): other = lax.ppermute(x, 'tgt', [(i, i ^ d) for i in range(n)])  6.07 us
    reduce_sum x3, other arithmetic, col_lse(): totals = jnp.sum(jnp.exp(shifted - peaks[None, :]), axis=0)  5.44 us
    reduce_sum x3, other arithmetic, row_lse(): totals = jnp.sum(jnp.exp(shifted - peaks[:, None]), axis=1)  5.14 us
  transfers between devices with their start and end apart: 13, of which 13 were waited for; matrix products, arithmetic and copies ran while one was open for 0% of the time, Pallas kernels for 0%

profile of v1, /device:TPU:1, one launch (start us, length us, event | category | flops | bytes accessed | tf_op | source)
XLA Modules:
  0.0 185.6 jit_solution(12199548133250486070)
XLA Ops:
  0.6 2.5 %convolution_convert_fusion = bf16[300,1024]{1,0:T(8,128)(2,1)S(1)} fusion(f32[300,300]{1,0:T(8,128)} %param.7, bf16[300,1024]{1,0:T(8,128)(2,1)} %param.5), kind=kOutput, calls=%fused_computation.15 | convolution fusion | flops 1106227200 | bytes 1588800 | tf_op jit(solution)/shard_map/dot_general | solution.py:67
  3.2 2.5 %fusion.35 = (f32[1024]{0:T(1024)S(1)}, f32[1024,2048]{1,0:T(8,128)S(1)}) fusion(bf16[300,1024]{1,0:T(8,128)(2,1)S(1)} %convolution_convert_fusion, bf16[300,2048]{1,0:T(8,128)(2,1)S(1)} %copy-done), kind=kOutput, calls=%fused_computation.87 | convolution fusion | flops 1260387328 | bytes 10235904 | tf_op jit(solution)/shard_map/dot_general | solution.py:70
  5.7 1.3 exponential_reduce_fusion.5
  7.0 18.7 %all_to_all.30 = f32[16,2,1024]{2,1,0:T(2,128)S(1)} all-to-all(f32[16,2,1024]{2,1,0:T(2,128)S(1)} %broadcast_in_dim.12), channel_id=1, replica_groups=mesh['src'=16,'tgt'=16] {'tgt'}, dimensions={0} | all-to-all | bytes 262144 | tf_op jit(solution)/shard_map/all_to_all | solution.py:14
  25.7 0.1 fusion.34
  25.9 0.6 add_reduce_fusion.3
  26.5 1.8 exponential_reduce_fusion.4
  28.5 15.1 %all_to_all.31 = f32[16,2,2048]{2,1,0:T(2,128)S(1)} all-to-all(f32[16,2,2048]{2,1,0:T(2,128)S(1)} %broadcast_in_dim.13), channel_id=1, replica_groups=mesh['src'=16,'tgt'=16] {'src'}, dimensions={0} | all-to-all | bytes 524288 | tf_op jit(solution)/shard_map/all_to_all | solution.py:14
  43.6 0.2 fusion.31
  43.9 0.6 add_reduce_fusion.2
  44.5 1.9 %exponential_reduce_fusion.3 = f32[1024]{0:T(1024)S(1)} fusion(f32[1024,2048]{1,0:T(8,128)S(1)} %get-tuple-element.22, f32[1024]{0:T(1024)S(1)} %add_reduce_fusion.2, f32[2048]{0:T(1024)S(1)} %add_subtract_fusion.2), kind=kLoop, calls=%fused_computation.4 | loop fusion | flops 6290432 | bytes 8404992 | tf_op jit(solution)/shard_map/reduce_sum | solution.py:22
  46.6 12.7 %all_to_all.32 = f32[16,2,1024]{2,1,0:T(2,128)S(1)} all-to-all(f32[16,2,1024]{2,1,0:T(2,128)S(1)} %broadcast_in_dim.14), channel_id=1, replica_groups=mesh['src'=16,'tgt'=16] {'tgt'}, dimensions={0} | all-to-all | bytes 262144 | tf_op jit(solution)/shard_map/all_to_all | solution.py:14
  59.2 0.1 fusion.33
  59.4 0.6 add_reduce_fusion.1
  60.1 1.8 exponential_reduce_fusion.2
  62.0 11.2 %all_to_all.33 = f32[16,2,2048]{2,1,0:T(2,128)S(1)} all-to-all(f32[16,2,2048]{2,1,0:T(2,128)S(1)} %broadcast_in_dim.15), channel_id=1, replica_groups=mesh['src'=16,'tgt'=16] {'src'}, dimensions={0} | all-to-all | bytes 524288 | tf_op jit(solution)/shard_map/all_to_all | solution.py:14
  73.2 0.2 fusion.30
  73.5 0.6 add_reduce_fusion
  74.2 1.9 %exponential_reduce_fusion.1 = f32[1024]{0:T(1024)S(1)} fusion(f32[1024,2048]{1,0:T(8,128)S(1)} %get-tuple-element.22, f32[1024]{0:T(1024)S(1)} %add_reduce_fusion, f32[2048]{0:T(1024)S(1)} %add_subtract_fusion.1), kind=kLoop, calls=%fused_computation.2 | loop fusion | flops 6290432 | bytes 8404992 | tf_op jit(solution)/shard_map/reduce_sum | solution.py:22
  76.2 12.7 %all_to_all.34 = f32[16,2,1024]{2,1,0:T(2,128)S(1)} all-to-all(f32[16,2,1024]{2,1,0:T(2,128)S(1)} %broadcast_in_dim.16), channel_id=1, replica_groups=mesh['src'=16,'tgt'=16] {'tgt'}, dimensions={0} | all-to-all | bytes 262144 | tf_op jit(solution)/shard_map/all_to_all | solution.py:14
  89.0 0.6 add_reduce_fusion.4
  89.7 1.8 exponential_reduce_fusion
  91.5 0.8 broadcast_in_dim.17
  92.3 3.5 %all-to-all-start.5 = ((f32[16,2,2048]{2,1,0:T(2,128)}), f32[16,2,2048]{2,1,0:T(2,128)S(1)}, u32[]{:S(2)}, u32[]{:S(2)}) async-start(f32[16,2,2048]{2,1,0:T(2,128)} %broadcast_in_dim.17), calls=%async_computation.5 | async-start | bytes 524288 | tf_op jit(solution)/shard_map/all_to_all | solution.py:14
  95.9 9.1 %all-to-all-done.5 = f32[16,2,2048]{2,1,0:T(2,128)S(1)} async-done(((f32[16,2,2048]{2,1,0:T(2,128)}), f32[16,2,2048]{2,1,0:T(2,128)S(1)}, u32[]{:S(2)}, u32[]{:S(2)}) %all-to-all-start.5) | async-done | bytes 262176 | tf_op jit(solution)/shard_map/all_to_all | solution.py:14
  105.0 0.2 fusion.29
  105.4 5.0 %fusion = f32[1024,300]{0,1:T(8,128)S(1)} fusion(bf16[300,2048]{1,0:T(8,128)(2,1)S(1)} %copy-done, f32[1024,2048]{1,0:T(8,128)} %copy-done.1, f32[2048]{0:T(1024)S(1)} %add_subtract_fusion, f32[1024]{0:T(1024)S(1)} %add_subtract_fusion.3), kind=kOutput, calls=%fused_computation.12 | convolution fusion | flops 1264582656 | bytes 10858496 | tf_op jit(solution)/shard_map/dot_general | solution.py:80
  110.4 1.1 convolution_bitcast_fusion
  111.8 13.2 %collective-permute-done = f32[152,300]{1,0:T(8,128)S(1)} collective-permute-done((f32[152,300]{1,0:T(8,128)S(1)}, f32[152,300]{1,0:T(8,128)S(1)}, u32[]{:S(2)}, u32[]{:S(2)}) %collective-permute-start) | collective-permute-done | bytes 182432 | tf_op jit(solution)/shard_map/ppermute | solution.py:54
  125.2 7.8 %collective-permute-done.1 = f32[76,300]{1,0:T(8,128)S(1)} collective-permute-done((f32[76,300]{1,0:T(8,128)S(1)}, f32[76,300]{1,0:T(8,128)S(1)}, u32[]{:S(2)}, u32[]{:S(2)}) %collective-permute-start.1) | collective-permute-done | bytes 91232 | tf_op jit(solution)/shard_map/ppermute | solution.py:54
  133.1 3.0 %collective-permute-done.2 = f32[38,300]{1,0:T(8,128)S(1)} collective-permute-done((f32[38,300]{1,0:T(8,128)S(1)}, f32[38,300]{1,0:T(8,128)S(1)}, u32[]{:S(2)}, u32[]{:S(2)}) %collective-permute-start.2) | collective-permute-done | bytes 45632 | tf_op jit(solution)/shard_map/ppermute | solution.py:54
  136.2 2.7 %collective-permute-start.3 = (f32[19,300]{1,0:T(8,128)S(1)}, f32[19,300]{1,0:T(8,128)S(1)}, u32[]{:S(2)}, u32[]{:S(2)}) collective-permute-start(f32[19,300]{1,0:T(8,128)S(1)} %slice_select_fusion.3), channel_id=1, source_target_pairs={{0,1},{1,0},{2,3},{3,2},{4,5},{5,4},{6,7},{7,6},{8,9},{9,8},{10,11... | collective-permute-start | bytes 68408 | tf_op jit(solution)/shard_map/ppermute | solution.py:54
  138.9 0.9 collective-permute-done.3
  139.8 0.4 collective-permute-start.4
  140.2 2.5 %collective-permute-done.4 = f32[19,300]{1,0:T(8,128)S(1)} collective-permute-done((f32[19,300]{1,0:T(8,128)S(1)}, f32[19,300]{1,0:T(8,128)S(1)}, u32[]{:S(2)}, u32[]{:S(2)}) %collective-permute-start.4) | collective-permute-done | bytes 22832 | tf_op jit(solution)/shard_map/ppermute | solution.py:36
  142.7 0.9 collective-permute-start.5
  143.6 3.4 %collective-permute-done.5 = f32[19,300]{1,0:T(8,128)S(1)} collective-permute-done((f32[19,300]{1,0:T(8,128)S(1)}, f32[19,300]{1,0:T(8,128)S(1)}, u32[]{:S(2)}, u32[]{:S(2)}) %collective-permute-start.5) | collective-permute-done | bytes 22832 | tf_op jit(solution)/shard_map/ppermute | solution.py:36
  147.0 2.8 %collective-permute-done.6 = f32[19,300]{1,0:T(8,128)S(1)} collective-permute-done((f32[19,300]{1,0:T(8,128)S(1)}, f32[19,300]{1,0:T(8,128)S(1)}, u32[]{:S(2)}, u32[]{:S(2)}) %collective-permute-start.6) | collective-permute-done | bytes 22832 | tf_op jit(solution)/shard_map/ppermute | solution.py:36
  149.8 0.5 collective-permute-start.7
  150.4 3.8 %collective-permute-done.7 = f32[19,300]{1,0:T(8,128)S(1)} collective-permute-done((f32[19,300]{1,0:T(8,128)S(1)}, f32[19,300]{1,0:T(8,128)S(1)}, u32[]{:S(2)}, u32[]{:S(2)}) %collective-permute-start.7) | collective-permute-done | bytes 22832 | tf_op jit(solution)/shard_map/ppermute | solution.py:36
  154.1 4.9 %collective-permute-start.8 = (f32[19,300]{1,0:T(8,128)S(1)}, f32[19,300]{1,0:T(8,128)S(1)}, u32[]{:S(2)}, u32[]{:S(2)}) collective-permute-start(f32[19,300]{1,0:T(8,128)S(1)} %add.146), channel_id=1, source_target_pairs={{0,1},{1,0},{2,3},{3,2},{4,5},{5,4},{6,7},{7,6},{8,9},{9,8},{10,11... | collective-permute-start | bytes 68408 | tf_op jit(solution)/shard_map/ppermute | solution.py:60
  159.1 0.9 collective-permute-done.8
  160.1 3.1 %collective-permute-done.9 = f32[38,300]{1,0:T(8,128)S(1)} collective-permute-done((f32[38,300]{1,0:T(8,128)S(1)}, f32[38,300]{1,0:T(8,128)S(1)}, u32[]{:S(2)}, u32[]{:S(2)}) %collective-permute-start.9) | collective-permute-done | bytes 45632 | tf_op jit(solution)/shard_map/ppermute | solution.py:60
  163.1 0.6 collective-permute-start.10
  163.7 8.1 %collective-permute-done.10 = f32[76,300]{1,0:T(8,128)S(1)} collective-permute-done((f32[76,300]{1,0:T(8,128)S(1)}, f32[76,300]{1,0:T(8,128)S(1)}, u32[]{:S(2)}, u32[]{:S(2)}) %collective-permute-start.10) | collective-permute-done | bytes 91232 | tf_op jit(solution)/shard_map/ppermute | solution.py:60
  171.9 0.4 collective-permute-start.11
  172.3 12.4 %collective-permute-done.11 = f32[152,300]{1,0:T(8,128)S(1)} collective-permute-done((f32[152,300]{1,0:T(8,128)S(1)}, f32[152,300]{1,0:T(8,128)S(1)}, u32[]{:S(2)}, u32[]{:S(2)}) %collective-permute-start.11) | collective-permute-done | bytes 182432 | tf_op jit(solution)/shard_map/ppermute | solution.py:60
  184.8 0.8 fusion.4
  (58 shorter events, 1.7 us)
Async XLA Ops:
  0.6 2.5 %copy-start = (bf16[300,2048]{1,0:T(8,128)(2,1)S(1)}, bf16[300,2048]{1,0:T(8,128)(2,1)}, u32[]{:S(2)}) copy-start(bf16[300,2048]{1,0:T(8,128)(2,1)} %param.6) | copy-start | bytes 3686404
  3.2 22.7 %copy-start.5 = (f32[1024]{0:T(1024)S(1)}, f32[1024]{0:T(1024)}, u32[]{:S(2)}) copy-start(f32[1024]{0:T(1024)} %param.8) | copy-start | bytes 12292
  5.7 84.0 %copy-start.1 = (f32[1024,2048]{1,0:T(8,128)}, f32[1024,2048]{1,0:T(8,128)S(1)}, u32[]{:S(2)}) copy-start(f32[1024,2048]{1,0:T(8,128)S(1)} %get-tuple-element.22) | copy-start | bytes 25165828
  25.9 18.0 %copy-start.3 = (f32[2048]{0:T(1024)S(1)}, f32[2048]{0:T(1024)}, u32[]{:S(2)}) copy-start(f32[2048]{0:T(1024)} %param.9) | copy-start | bytes 24580
  89.0 16.3 %copy-start.4 = (f32[1024]{0:T(1024)}, f32[1024]{0:T(1024)S(1)}, u32[]{:S(2)}) copy-start(f32[1024]{0:T(1024)S(1)} %add_subtract_fusion.3) | copy-start | bytes 12292
  92.3 12.6 %all-to-all-start.5 = ((f32[16,2,2048]{2,1,0:T(2,128)}), f32[16,2,2048]{2,1,0:T(2,128)S(1)}, u32[]{:S(2)}, u32[]{:S(2)}) async-start(f32[16,2,2048]{2,1,0:T(2,128)} %broadcast_in_dim.17), calls=%async_computation.5 | async-start | bytes 524288 | tf_op jit(solution)/shard_map/all_to_all | solution.py:14
  105.3 5.1 %copy-start.6 = (f32[2048]{0:T(1024)}, f32[2048]{0:T(1024)S(1)}, u32[]{:S(2)}) copy-start(f32[2048]{0:T(1024)S(1)} %add_subtract_fusion) | copy-start | bytes 24580
  105.4 5.1 %copy-start.2 = (bf16[300,1024]{1,0:T(8,128)(2,1)S(1)}, bf16[300,1024]{1,0:T(8,128)(2,1)}, u32[]{:S(2)}) copy-start(bf16[300,1024]{1,0:T(8,128)(2,1)} %param.5) | copy-start | bytes 1843204
  111.6 13.4 %collective-permute-start = (f32[152,300]{1,0:T(8,128)S(1)}, f32[152,300]{1,0:T(8,128)S(1)}, u32[]{:S(2)}, u32[]{:S(2)}) collective-permute-start(f32[152,300]{1,0:T(8,128)S(1)} %slice_select_fusion), channel_id=1, source_target_pairs={{0,8},{1,9},{2,10},{3,11},{4,12},{5,13},{6,14},{7,15},{8,0},{9,1},... | collective-permute-start | bytes 547208 | tf_op jit(solution)/shard_map/ppermute | solution.py:54
  125.1 7.9 %collective-permute-start.1 = (f32[76,300]{1,0:T(8,128)S(1)}, f32[76,300]{1,0:T(8,128)S(1)}, u32[]{:S(2)}, u32[]{:S(2)}) collective-permute-start(f32[76,300]{1,0:T(8,128)S(1)} %slice_select_fusion.1), channel_id=1, source_target_pairs={{0,4},{1,5},{2,6},{3,7},{4,0},{5,1},{6,2},{7,3},{8,12},{9,13},{10,... | collective-permute-start | bytes 273608 | tf_op jit(solution)/shard_map/ppermute | solution.py:54
  133.0 3.2 %collective-permute-start.2 = (f32[38,300]{1,0:T(8,128)S(1)}, f32[38,300]{1,0:T(8,128)S(1)}, u32[]{:S(2)}, u32[]{:S(2)}) collective-permute-start(f32[38,300]{1,0:T(8,128)S(1)} %slice_select_fusion.2), channel_id=1, source_target_pairs={{0,2},{1,3},{2,0},{3,1},{4,6},{5,7},{6,4},{7,5},{8,10},{9,11},{10,... | collective-permute-start | bytes 136808 | tf_op jit(solution)/shard_map/ppermute | solution.py:54
  136.2 3.6 %collective-permute-start.3 = (f32[19,300]{1,0:T(8,128)S(1)}, f32[19,300]{1,0:T(8,128)S(1)}, u32[]{:S(2)}, u32[]{:S(2)}) collective-permute-start(f32[19,300]{1,0:T(8,128)S(1)} %slice_select_fusion.3), channel_id=1, source_target_pairs={{0,1},{1,0},{2,3},{3,2},{4,5},{5,4},{6,7},{7,6},{8,9},{9,8},{10,11... | collective-permute-start | bytes 68408 | tf_op jit(solution)/shard_map/ppermute | solution.py:54
  139.8 2.9 %collective-permute-start.4 = (f32[19,300]{1,0:T(8,128)S(1)}, f32[19,300]{1,0:T(8,128)S(1)}, u32[]{:S(2)}, u32[]{:S(2)}) collective-permute-start(f32[19,300]{1,0:T(8,128)S(1)} %select_add_fusion.3), channel_id=1, source_target_pairs={{0,16},{16,0},{32,48},{48,32},{64,80},{80,64},{96,112},{112,96},{1... | collective-permute-start | bytes 68408 | tf_op jit(solution)/shard_map/ppermute | solution.py:36
  142.7 4.3 %collective-permute-start.5 = (f32[19,300]{1,0:T(8,128)S(1)}, f32[19,300]{1,0:T(8,128)S(1)}, u32[]{:S(2)}, u32[]{:S(2)}) collective-permute-start(f32[19,300]{1,0:T(8,128)S(1)} %add.143), channel_id=1, source_target_pairs={{0,32},{16,48},{32,0},{48,16},{64,96},{80,112},{96,64},{112,80},{1... | collective-permute-start | bytes 68408 | tf_op jit(solution)/shard_map/ppermute | solution.py:36
  147.0 2.8 %collective-permute-start.6 = (f32[19,300]{1,0:T(8,128)S(1)}, f32[19,300]{1,0:T(8,128)S(1)}, u32[]{:S(2)}, u32[]{:S(2)}) collective-permute-start(f32[19,300]{1,0:T(8,128)S(1)} %add.144), channel_id=1, source_target_pairs={{0,64},{16,80},{32,96},{48,112},{64,0},{80,16},{96,32},{112,48},{1... | collective-permute-start | bytes 68408 | tf_op jit(solution)/shard_map/ppermute | solution.py:36
  149.8 4.3 %collective-permute-start.7 = (f32[19,300]{1,0:T(8,128)S(1)}, f32[19,300]{1,0:T(8,128)S(1)}, u32[]{:S(2)}, u32[]{:S(2)}) collective-permute-start(f32[19,300]{1,0:T(8,128)S(1)} %add.145), channel_id=1, source_target_pairs={{0,128},{16,144},{32,160},{48,176},{64,192},{80,208},{96,224},{112... | collective-permute-start | bytes 68408 | tf_op jit(solution)/shard_map/ppermute | solution.py:36
  154.1 5.8 %collective-permute-start.8 = (f32[19,300]{1,0:T(8,128)S(1)}, f32[19,300]{1,0:T(8,128)S(1)}, u32[]{:S(2)}, u32[]{:S(2)}) collective-permute-start(f32[19,300]{1,0:T(8,128)S(1)} %add.146), channel_id=1, source_target_pairs={{0,1},{1,0},{2,3},{3,2},{4,5},{5,4},{6,7},{7,6},{8,9},{9,8},{10,11... | collective-permute-start | bytes 68408 | tf_op jit(solution)/shard_map/ppermute | solution.py:60
  160.0 3.2 %collective-permute-start.9 = (f32[38,300]{1,0:T(8,128)S(1)}, f32[38,300]{1,0:T(8,128)S(1)}, u32[]{:S(2)}, u32[]{:S(2)}) collective-permute-start(f32[38,300]{1,0:T(8,128)S(1)} %maximum_select_fusion.2), channel_id=1, source_target_pairs={{0,2},{1,3},{2,0},{3,1},{4,6},{5,7},{6,4},{7,5},{8,10},{9,11},{10,... | collective-permute-start | bytes 136808 | tf_op jit(solution)/shard_map/ppermute | solution.py:60
  163.1 8.7 %collective-permute-start.10 = (f32[76,300]{1,0:T(8,128)S(1)}, f32[76,300]{1,0:T(8,128)S(1)}, u32[]{:S(2)}, u32[]{:S(2)}) collective-permute-start(f32[76,300]{1,0:T(8,128)S(1)} %maximum_select_fusion.1), channel_id=1, source_target_pairs={{0,4},{1,5},{2,6},{3,7},{4,0},{5,1},{6,2},{7,3},{8,12},{9,13},{10,... | collective-permute-start | bytes 273608 | tf_op jit(solution)/shard_map/ppermute | solution.py:60
  171.9 12.9 %collective-permute-start.11 = (f32[152,300]{1,0:T(8,128)S(1)}, f32[152,300]{1,0:T(8,128)S(1)}, u32[]{:S(2)}, u32[]{:S(2)}) collective-permute-start(f32[152,300]{1,0:T(8,128)S(1)} %maximum_select_fusion), channel_id=1, source_target_pairs={{0,8},{1,9},{2,10},{3,11},{4,12},{5,13},{6,14},{7,15},{8,0},{9,1},... | collective-permute-start | bytes 547208 | tf_op jit(solution)/shard_map/ppermute | solution.py:60

commit v2 on v1

--- a/solution.py
+++ b/solution.py
@@ -39,28 +39,15 @@
 
 
 def sum_all(c):
-    n = lax.axis_size("tgt")
-    rows = c.shape[0]
-    padded = -(-rows // n) * n
-    x = jnp.pad(c, ((0, padded - rows), (0, 0)))
-    idx = lax.axis_index("tgt")
-    d = n // 2
-    while d >= 1:
-        half = x.shape[0] // 2
-        lo, hi = x[:half], x[half:]
-        upper = (idx // d) % 2 == 1
-        send = jnp.where(upper, lo, hi)
-        keep = jnp.where(upper, hi, lo)
-        x = keep + lax.ppermute(send, "tgt", [(i, i ^ d) for i in range(n)])
-        d //= 2
-    x = butterfly_sum(x, "src")
-    d = 1
-    while d < n:
-        upper = (idx // d) % 2 == 1
-        other = lax.ppermute(x, "tgt", [(i, i ^ d) for i in range(n)])
-        x = jnp.where(upper, jnp.concatenate([other, x]), jnp.concatenate([x, other]))
-        d *= 2
-    return x[:rows]
+    axes = ("src", "tgt")
+    n = lax.axis_size(axes)
+    rows, cols = c.shape
+    k = rows * cols
+    per = -(-k // n)
+    x = jnp.pad(c.reshape(-1), (0, per * n - k)).reshape(n, per)
+    x = jnp.sum(lax.all_to_all(x, axes, 0, 0, tiled=False), axis=0)
+    x = lax.all_to_all(jnp.broadcast_to(x[None], (n, per)), axes, 0, 0, tiled=False).reshape(-1)[:k]
+    return x.reshape(rows, cols)
 
 
 def per_device(src_emb_t, tgt_emb_t, core, src_logw, tgt_logw):

time: 186 us -> 159 us (0.85)
  waiting for transfers between devices: 71 us -> 0 us
  blocking collectives: 70.3 us -> 130 us
  starting transfers between devices: 14.4 us -> 0 us
  matrix products: 11.2 us -> 7.83 us
  local copies, waits for them, and re-layouts: 1.15 us -> 3.55 us
    ppermute x12 -> x0, waiting for transfers between devices: 61.9 us -> none  [the longest x4 24.9 us: sum_all(): x = keep + lax.ppermute(send, 'tgt', [(i, i ^ d) for i in range(n)])]
    all_to_all x0 -> x2, blocking collectives: none -> 48.6 us  [the longest x1 24.6 us: sum_all(): x = jnp.sum(lax.all_to_all(x, axes, 0, 0, tiled=False), axis=0)]
    all_to_all x5 -> x6, blocking collectives: 70.3 us -> 81.5 us  [merge_lse(): got = lax.all_to_all(sent, axis, 0, 0, tiled=False)]
    ppermute x12 -> x0, starting transfers between devices: 10.9 us -> none  [the longest x4 6.07 us: sum_all(): other = lax.ppermute(x, 'tgt', [(i, i ^ d) for i in range(n)])]
    all_to_all x1 -> x0, waiting for transfers between devices: 9.07 us -> none  [merge_lse(): got = lax.all_to_all(sent, axis, 0, 0, tiled=False)]
    all_to_all x1 -> x0, starting transfers between devices: 3.53 us -> none  [merge_lse(): got = lax.all_to_all(sent, axis, 0, 0, tiled=False)]
    dot_general x1, matrix products: 5.05 us -> 1.7 us  [per_device(): lax.dot_general(plan, tgt_emb_t, (((1,), (1,)), ((), ())), preferred_elem...]
  transfers between devices with their start and end apart: 13 -> 0, of which waited for: 13 -> 0; matrix products, arithmetic and copies ran while one was open for 0% -> 0% of each run, Pallas kernels for 0% -> 0%
where the time goes in v2:
time: 159 us
  blocking collectives  130 us (82%)
  other arithmetic  16.6 us (10%)
  matrix products  7.83 us (5%)
  local copies, waits for them, and re-layouts  3.55 us (2%)
    all_to_all x6, blocking collectives, merge_lse(): got = lax.all_to_all(sent, axis, 0, 0, tiled=False)  81.5 us
    all_to_all x1, blocking collectives, sum_all(): x = jnp.sum(lax.all_to_all(x, axes, 0, 0, tiled=False), axis=0)  24.6 us
    all_to_all x1, blocking collectives, sum_all(): lax.all_to_all(jnp.broadcast_to(x[None], (n, per)), axes, 0, 0, tiled=False)  24 us
    reduce_sum x3, other arithmetic, col_lse(): totals = jnp.sum(jnp.exp(shifted - peaks[None, :]), axis=0)  5.44 us
    reduce_sum x3, other arithmetic, row_lse(): totals = jnp.sum(jnp.exp(shifted - peaks[:, None]), axis=1)  5.14 us

profile of v2, /device:TPU:1, one launch (start us, length us, event | category | flops | bytes accessed | tf_op | source)
XLA Modules:
  0.0 159.1 jit_solution(1066378116920329145)
XLA Ops:
  0.6 0.0 copy-start
  0.6 2.5 %convolution_convert_fusion = bf16[300,1024]{1,0:T(8,128)(2,1)S(1)} fusion(f32[300,300]{1,0:T(8,128)} %param.7, bf16[300,1024]{1,0:T(8,128)(2,1)} %param.5), kind=kOutput, calls=%fused_computation.15 | convolution fusion | flops 1106227200 | bytes 1588800 | tf_op jit(solution)/shard_map/dot_general | solution.py:54
  3.2 0.0 copy-start.4
  3.2 2.5 %fusion.33 = (f32[1024]{0:T(1024)S(1)}, f32[1024,2048]{1,0:T(8,128)S(1)}) fusion(bf16[300,1024]{1,0:T(8,128)(2,1)S(1)} %convolution_convert_fusion, bf16[300,2048]{1,0:T(8,128)(2,1)S(1)} %copy-done), kind=kOutput, calls=%fused_computation.72 | convolution fusion | flops 1260387328 | bytes 10235904 | tf_op jit(solution)/shard_map/dot_general | solution.py:57
  5.7 1.3 exponential_reduce_fusion.5
  7.0 18.7 %all_to_all.46 = f32[16,2,1024]{2,1,0:T(2,128)S(1)} all-to-all(f32[16,2,1024]{2,1,0:T(2,128)S(1)} %broadcast_in_dim.14), channel_id=1, replica_groups=mesh['src'=16,'tgt'=16] {'tgt'}, dimensions={0} | all-to-all | bytes 262144 | tf_op jit(solution)/shard_map/all_to_all | solution.py:14
  25.7 0.1 fusion.32
  25.9 0.6 add_reduce_fusion.3
  26.5 1.8 %exponential_reduce_fusion.4 = f32[2048]{0:T(1024)S(1)} fusion(f32[1024,2048]{1,0:T(8,128)S(1)} %get-tuple-element.22, f32[2048]{0:T(1024)S(1)} %add_reduce_fusion.3, f32[1024]{0:T(1024)S(1)} %add_subtract_fusion.5), kind=kLoop, calls=%fused_computation.5 | loop fusion | flops 6289408 | bytes 8409088 | tf_op jit(solution)/shard_map/reduce_sum | solution.py:28
  28.4 0.1 broadcast_in_dim.15
  28.5 15.1 %all_to_all.47 = f32[16,2,2048]{2,1,0:T(2,128)S(1)} all-to-all(f32[16,2,2048]{2,1,0:T(2,128)S(1)} %broadcast_in_dim.15), channel_id=1, replica_groups=mesh['src'=16,'tgt'=16] {'src'}, dimensions={0} | all-to-all | bytes 524288 | tf_op jit(solution)/shard_map/all_to_all | solution.py:14
  43.6 0.2 fusion.29
  43.8 0.1 fusion.14
  43.9 0.6 add_reduce_fusion.2
  44.5 1.9 %exponential_reduce_fusion.3 = f32[1024]{0:T(1024)S(1)} fusion(f32[1024,2048]{1,0:T(8,128)S(1)} %get-tuple-element.22, f32[1024]{0:T(1024)S(1)} %add_reduce_fusion.2, f32[2048]{0:T(1024)S(1)} %add_subtract_fusion.2), kind=kLoop, calls=%fused_computation.4 | loop fusion | flops 6290432 | bytes 8404992 | tf_op jit(solution)/shard_map/reduce_sum | solution.py:22
  46.5 12.7 %all_to_all.48 = f32[16,2,1024]{2,1,0:T(2,128)S(1)} all-to-all(f32[16,2,1024]{2,1,0:T(2,128)S(1)} %broadcast_in_dim.16), channel_id=1, replica_groups=mesh['src'=16,'tgt'=16] {'tgt'}, dimensions={0} | all-to-all | bytes 262144 | tf_op jit(solution)/shard_map/all_to_all | solution.py:14
  59.2 0.1 fusion.31
  59.4 0.6 add_reduce_fusion.1
  60.0 1.8 %exponential_reduce_fusion.2 = f32[2048]{0:T(1024)S(1)} fusion(f32[1024,2048]{1,0:T(8,128)S(1)} %get-tuple-element.22, f32[2048]{0:T(1024)S(1)} %add_reduce_fusion.1, f32[1024]{0:T(1024)S(1)} %add_subtract_fusion.4), kind=kLoop, calls=%fused_computation.3 | loop fusion | flops 6289408 | bytes 8409088 | tf_op jit(solution)/shard_map/reduce_sum | solution.py:28
  61.9 0.1 broadcast_in_dim.17
  62.0 11.2 %all_to_all.49 = f32[16,2,2048]{2,1,0:T(2,128)S(1)} all-to-all(f32[16,2,2048]{2,1,0:T(2,128)S(1)} %broadcast_in_dim.17), channel_id=1, replica_groups=mesh['src'=16,'tgt'=16] {'src'}, dimensions={0} | all-to-all | bytes 524288 | tf_op jit(solution)/shard_map/all_to_all | solution.py:14
  73.2 0.2 fusion.28
  73.4 0.1 fusion.10
  73.5 0.6 add_reduce_fusion
  74.1 1.9 %exponential_reduce_fusion.1 = f32[1024]{0:T(1024)S(1)} fusion(f32[1024,2048]{1,0:T(8,128)S(1)} %get-tuple-element.22, f32[1024]{0:T(1024)S(1)} %add_reduce_fusion, f32[2048]{0:T(1024)S(1)} %add_subtract_fusion.1), kind=kLoop, calls=%fused_computation.2 | loop fusion | flops 6290432 | bytes 8404992 | tf_op jit(solution)/shard_map/reduce_sum | solution.py:22
  76.2 12.7 %all_to_all.50 = f32[16,2,1024]{2,1,0:T(2,128)S(1)} all-to-all(f32[16,2,1024]{2,1,0:T(2,128)S(1)} %broadcast_in_dim.18), channel_id=1, replica_groups=mesh['src'=16,'tgt'=16] {'tgt'}, dimensions={0} | all-to-all | bytes 262144 | tf_op jit(solution)/shard_map/all_to_all | solution.py:14
  88.8 0.1 fusion.30
  89.0 0.0 copy-start.3
  89.0 0.6 add_reduce_fusion.4
  89.7 1.8 %exponential_reduce_fusion = f32[2048]{0:T(1024)S(1)} fusion(f32[1024,2048]{1,0:T(8,128)S(1)} %get-tuple-element.22, f32[2048]{0:T(1024)S(1)} %add_reduce_fusion.4, f32[1024]{0:T(1024)S(1)} %add_subtract_fusion.3), kind=kLoop, calls=%fused_computation.1 | loop fusion | flops 6289408 | bytes 8409088 | tf_op jit(solution)/shard_map/reduce_sum | solution.py:28
  91.5 0.1 broadcast_in_dim.19
  91.6 11.2 %all_to_all.51 = f32[16,2,2048]{2,1,0:T(2,128)S(1)} all-to-all(f32[16,2,2048]{2,1,0:T(2,128)S(1)} %broadcast_in_dim.19), channel_id=1, replica_groups=mesh['src'=16,'tgt'=16] {'src'}, dimensions={0} | all-to-all | bytes 524288 | tf_op jit(solution)/shard_map/all_to_all | solution.py:14
  102.8 0.2 fusion.27
  103.0 0.1 fusion.6
  103.2 0.0 copy-start.5
  103.2 0.0 copy-start.1
  103.2 1.7 %fusion = f32[1024,300]{0,1:T(8,128)S(1)} fusion(bf16[300,2048]{1,0:T(8,128)(2,1)S(1)} %copy-done, f32[1024,2048]{1,0:T(8,128)S(1)} %get-tuple-element.22, f32[2048]{0:T(1024)S(1)} %add_subtract_fusion, f32[1024]{0:T(1024)S(1)} %add_subtract_fusion.3), kind=kOutput, calls=%fused_computation.12 | convolution fusion | flops 1264582656 | bytes 10858496 | tf_op jit(solution)/shard_map/dot_general | solution.py:67
  104.9 1.1 convolution_bitcast_fusion
  106.0 0.2 copy.37
  106.2 0.5 reshape.50
  106.7 0.6 all_to_all.37
  107.4 24.6 %all_to_all.52 = f32[256,1,352]{2,1,0:T(1,128)S(1)} all-to-all(f32[256,1,352]{2,1,0:T(1,128)S(1)} %all_to_all.37), channel_id=1, replica_groups=mesh['src'=16,'tgt'=16] {'src','tgt'}, dimensions={0} | all-to-all | bytes 720896 | tf_op jit(solution)/shard_map/all_to_all | solution.py:48
  132.0 0.3 reduce_sum.129
  132.3 0.2 broadcast_in_dim.20
  132.5 24.0 %all_to_all.53 = f32[256,1,352]{2,1,0:T(1,128)S(1)} all-to-all(f32[256,1,352]{2,1,0:T(1,128)S(1)} %broadcast_in_dim.20), channel_id=1, replica_groups=mesh['src'=16,'tgt'=16] {'src','tgt'}, dimensions={0} | all-to-all | bytes 720896 | tf_op jit(solution)/shard_map/all_to_all | solution.py:49
  156.5 0.9 reduce.7
  157.5 0.3 reshape.51
  157.8 1.2 mul.35
  (27 shorter events, 0.4 us)
Async XLA Ops:
  0.6 2.5 %copy-start = (bf16[300,2048]{1,0:T(8,128)(2,1)S(1)}, bf16[300,2048]{1,0:T(8,128)(2,1)}, u32[]{:S(2)}) copy-start(bf16[300,2048]{1,0:T(8,128)(2,1)} %param.6) | copy-start | bytes 3686404
  3.2 22.7 %copy-start.4 = (f32[1024]{0:T(1024)S(1)}, f32[1024]{0:T(1024)}, u32[]{:S(2)}) copy-start(f32[1024]{0:T(1024)} %param.8) | copy-start | bytes 12292
  25.9 18.0 %copy-start.2 = (f32[2048]{0:T(1024)S(1)}, f32[2048]{0:T(1024)}, u32[]{:S(2)}) copy-start(f32[2048]{0:T(1024)} %param.9) | copy-start | bytes 24580
  89.0 14.1 %copy-start.3 = (f32[1024]{0:T(1024)}, f32[1024]{0:T(1024)S(1)}, u32[]{:S(2)}) copy-start(f32[1024]{0:T(1024)S(1)} %add_subtract_fusion.3) | copy-start | bytes 12292
  103.2 1.7 %copy-start.5 = (f32[2048]{0:T(1024)}, f32[2048]{0:T(1024)S(1)}, u32[]{:S(2)}) copy-start(f32[2048]{0:T(1024)S(1)} %add_subtract_fusion) | copy-start | bytes 24580
  103.2 1.7 %copy-start.1 = (bf16[300,1024]{1,0:T(8,128)(2,1)S(1)}, bf16[300,1024]{1,0:T(8,128)(2,1)}, u32[]{:S(2)}) copy-start(bf16[300,1024]{1,0:T(8,128)(2,1)} %param.5) | copy-start | bytes 1843204

commit v3 on v2

--- a/solution.py
+++ b/solution.py
@@ -38,16 +38,17 @@
     return x
 
 
-def sum_all(c):
-    axes = ("src", "tgt")
-    n = lax.axis_size(axes)
+def sum_all(c, scale):
+    n = lax.axis_size("tgt")
+    m = lax.axis_size("src")
     rows, cols = c.shape
     k = rows * cols
     per = -(-k // n)
     x = jnp.pad(c.reshape(-1), (0, per * n - k)).reshape(n, per)
-    x = jnp.sum(lax.all_to_all(x, axes, 0, 0, tiled=False), axis=0)
-    x = lax.all_to_all(jnp.broadcast_to(x[None], (n, per)), axes, 0, 0, tiled=False).reshape(-1)[:k]
-    return x.reshape(rows, cols)
+    x = jnp.sum(lax.all_to_all(x, "tgt", 0, 0, tiled=True), axis=0)
+    x = jnp.sum(lax.all_to_all(jnp.broadcast_to(x[None], (m, per)), "src", 0, 0, tiled=True), axis=0) * scale
+    x = lax.all_to_all(jnp.broadcast_to(x[None], (n, per)), "tgt", 0, 0, tiled=True)
+    return x.reshape(-1)[:k].reshape(rows, cols)
 
 
 def per_device(src_emb_t, tgt_emb_t, core, src_logw, tgt_logw):
@@ -68,7 +69,7 @@
         plan, tgt_emb_t, (((1,), (1,)), ((), ())), preferred_element_type=jnp.float32
     )
     partial_core = jnp.dot(src_emb_t.astype(jnp.float32), panel, precision=lax.Precision.HIGHEST)
-    next_core = sum_all(partial_core) * (D / total_words)
+    next_core = sum_all(partial_core, D / total_words)
     return (src_pot, tgt_pot, next_core)
 
 

time: 159 us -> 157 us (0.987)
  blocking collectives: 130 us -> 128 us
    all_to_all x2 -> x3, blocking collectives: 48.6 us -> 47 us  [the longest x1 17.5 us: sum_all(): x = jnp.sum(lax.all_to_all(x, 'tgt', 0, 0, tiled=True), axis=0)]
where the time goes in v3:
time: 157 us
  blocking collectives  128 us (82%)
  other arithmetic  16.6 us (11%)
  matrix products  7.83 us (5%)
  local copies, waits for them, and re-layouts  3 us (2%)
    all_to_all x6, blocking collectives, merge_lse(): got = lax.all_to_all(sent, axis, 0, 0, tiled=False)  81.5 us
    all_to_all x1, blocking collectives, sum_all(): x = jnp.sum(lax.all_to_all(x, 'tgt', 0, 0, tiled=True), axis=0)  17.5 us
    all_to_all x1, blocking collectives, sum_all(): lax.all_to_all(jnp.broadcast_to(x[None], (n, per)), 'tgt', 0, 0, tiled=True)  16.8 us
    all_to_all x1, blocking collectives, sum_all(): lax.all_to_all(jnp.broadcast_to(x[None], (m, per)), 'src', 0, 0, tiled=True)  12.8 us
    reduce_sum x3, other arithmetic, col_lse(): totals = jnp.sum(jnp.exp(shifted - peaks[None, :]), axis=0)  5.44 us
    reduce_sum x3, other arithmetic, row_lse(): totals = jnp.sum(jnp.exp(shifted - peaks[:, None]), axis=1)  5.14 us

profile of v3, /device:TPU:1, one launch (start us, length us, event | category | flops | bytes accessed | tf_op | source)
XLA Modules:
  0.0 156.9 jit_solution(18444454997028661814)
XLA Ops:
  0.6 0.0 copy-start
  0.6 2.5 %convolution_convert_fusion = bf16[300,1024]{1,0:T(8,128)(2,1)S(1)} fusion(f32[300,300]{1,0:T(8,128)} %param.7, bf16[300,1024]{1,0:T(8,128)(2,1)} %param.5), kind=kOutput, calls=%fused_computation.15 | convolution fusion | flops 1106227200 | bytes 1588800 | tf_op jit(solution)/shard_map/dot_general | solution.py:55
  3.2 2.5 %fusion.33 = (f32[1024]{0:T(1024)S(1)}, f32[1024,2048]{1,0:T(8,128)S(1)}) fusion(bf16[300,1024]{1,0:T(8,128)(2,1)S(1)} %convolution_convert_fusion, bf16[300,2048]{1,0:T(8,128)(2,1)S(1)} %copy-done), kind=kOutput, calls=%fused_computation.72 | convolution fusion | flops 1260387328 | bytes 10235904 | tf_op jit(solution)/shard_map/dot_general | solution.py:58
  5.7 1.3 exponential_reduce_fusion.5
  7.0 18.7 %all_to_all.52 = f32[16,2,1024]{2,1,0:T(2,128)S(1)} all-to-all(f32[16,2,1024]{2,1,0:T(2,128)S(1)} %broadcast_in_dim.16), channel_id=1, replica_groups=mesh['src'=16,'tgt'=16] {'tgt'}, dimensions={0} | all-to-all | bytes 262144 | tf_op jit(solution)/shard_map/all_to_all | solution.py:14
  25.7 0.1 fusion.32
  25.9 0.6 add_reduce_fusion.3
  26.5 1.8 %exponential_reduce_fusion.4 = f32[2048]{0:T(1024)S(1)} fusion(f32[1024,2048]{1,0:T(8,128)S(1)} %get-tuple-element.22, f32[2048]{0:T(1024)S(1)} %add_reduce_fusion.3, f32[1024]{0:T(1024)S(1)} %add_subtract_fusion.5), kind=kLoop, calls=%fused_computation.5 | loop fusion | flops 6289408 | bytes 8409088 | tf_op jit(solution)/shard_map/reduce_sum | solution.py:28
  28.4 0.1 broadcast_in_dim.17
  28.5 15.1 %all_to_all.53 = f32[16,2,2048]{2,1,0:T(2,128)S(1)} all-to-all(f32[16,2,2048]{2,1,0:T(2,128)S(1)} %broadcast_in_dim.17), channel_id=1, replica_groups=mesh['src'=16,'tgt'=16] {'src'}, dimensions={0} | all-to-all | bytes 524288 | tf_op jit(solution)/shard_map/all_to_all | solution.py:14
  43.6 0.2 fusion.29
  43.8 0.1 fusion.14
  43.9 0.6 add_reduce_fusion.2
  44.5 1.9 %exponential_reduce_fusion.3 = f32[1024]{0:T(1024)S(1)} fusion(f32[1024,2048]{1,0:T(8,128)S(1)} %get-tuple-element.22, f32[1024]{0:T(1024)S(1)} %add_reduce_fusion.2, f32[2048]{0:T(1024)S(1)} %add_subtract_fusion.2), kind=kLoop, calls=%fused_computation.4 | loop fusion | flops 6290432 | bytes 8404992 | tf_op jit(solution)/shard_map/reduce_sum | solution.py:22
  46.5 12.7 %all_to_all.54 = f32[16,2,1024]{2,1,0:T(2,128)S(1)} all-to-all(f32[16,2,1024]{2,1,0:T(2,128)S(1)} %broadcast_in_dim.18), channel_id=1, replica_groups=mesh['src'=16,'tgt'=16] {'tgt'}, dimensions={0} | all-to-all | bytes 262144 | tf_op jit(solution)/shard_map/all_to_all | solution.py:14
  59.2 0.1 fusion.31
  59.4 0.6 add_reduce_fusion.1
  60.0 1.8 %exponential_reduce_fusion.2 = f32[2048]{0:T(1024)S(1)} fusion(f32[1024,2048]{1,0:T(8,128)S(1)} %get-tuple-element.22, f32[2048]{0:T(1024)S(1)} %add_reduce_fusion.1, f32[1024]{0:T(1024)S(1)} %add_subtract_fusion.4), kind=kLoop, calls=%fused_computation.3 | loop fusion | flops 6289408 | bytes 8409088 | tf_op jit(solution)/shard_map/reduce_sum | solution.py:28
  61.9 0.1 broadcast_in_dim.19
  62.0 11.2 %all_to_all.55 = f32[16,2,2048]{2,1,0:T(2,128)S(1)} all-to-all(f32[16,2,2048]{2,1,0:T(2,128)S(1)} %broadcast_in_dim.19), channel_id=1, replica_groups=mesh['src'=16,'tgt'=16] {'src'}, dimensions={0} | all-to-all | bytes 524288 | tf_op jit(solution)/shard_map/all_to_all | solution.py:14
  73.2 0.2 fusion.28
  73.4 0.1 fusion.10
  73.5 0.6 add_reduce_fusion
  74.1 1.9 %exponential_reduce_fusion.1 = f32[1024]{0:T(1024)S(1)} fusion(f32[1024,2048]{1,0:T(8,128)S(1)} %get-tuple-element.22, f32[1024]{0:T(1024)S(1)} %add_reduce_fusion, f32[2048]{0:T(1024)S(1)} %add_subtract_fusion.1), kind=kLoop, calls=%fused_computation.2 | loop fusion | flops 6290432 | bytes 8404992 | tf_op jit(solution)/shard_map/reduce_sum | solution.py:22
  76.2 12.7 %all_to_all.56 = f32[16,2,1024]{2,1,0:T(2,128)S(1)} all-to-all(f32[16,2,1024]{2,1,0:T(2,128)S(1)} %broadcast_in_dim.20), channel_id=1, replica_groups=mesh['src'=16,'tgt'=16] {'tgt'}, dimensions={0} | all-to-all | bytes 262144 | tf_op jit(solution)/shard_map/all_to_all | solution.py:14
  88.8 0.1 fusion.30
  89.0 0.0 copy-start.3
  89.0 0.6 add_reduce_fusion.4
  89.7 1.8 %exponential_reduce_fusion = f32[2048]{0:T(1024)S(1)} fusion(f32[1024,2048]{1,0:T(8,128)S(1)} %get-tuple-element.22, f32[2048]{0:T(1024)S(1)} %add_reduce_fusion.4, f32[1024]{0:T(1024)S(1)} %add_subtract_fusion.3), kind=kLoop, calls=%fused_computation.1 | loop fusion | flops 6289408 | bytes 8409088 | tf_op jit(solution)/shard_map/reduce_sum | solution.py:28
  91.5 0.1 broadcast_in_dim.21
  91.6 11.2 %all_to_all.57 = f32[16,2,2048]{2,1,0:T(2,128)S(1)} all-to-all(f32[16,2,2048]{2,1,0:T(2,128)S(1)} %broadcast_in_dim.21), channel_id=1, replica_groups=mesh['src'=16,'tgt'=16] {'src'}, dimensions={0} | all-to-all | bytes 524288 | tf_op jit(solution)/shard_map/all_to_all | solution.py:14
  102.8 0.2 fusion.27
  103.0 0.1 fusion.6
  103.2 0.0 copy-start.5
  103.2 0.0 copy-start.1
  103.2 1.7 %fusion = f32[1024,300]{0,1:T(8,128)S(1)} fusion(bf16[300,2048]{1,0:T(8,128)(2,1)S(1)} %copy-done, f32[1024,2048]{1,0:T(8,128)S(1)} %get-tuple-element.22, f32[2048]{0:T(1024)S(1)} %add_subtract_fusion, f32[1024]{0:T(1024)S(1)} %add_subtract_fusion.3), kind=kOutput, calls=%fused_computation.12 | convolution fusion | flops 1264582656 | bytes 10858496 | tf_op jit(solution)/shard_map/dot_general | solution.py:68
  104.9 1.1 convolution_bitcast_fusion
  106.0 0.2 copy.37
  106.2 0.8 all_to_all.42
  107.0 17.5 %all_to_all.58 = f32[16,1,5625]{2,1,0:T(1,128)S(1)} all-to-all(f32[16,1,5625]{2,1,0:T(1,128)S(1)} %all_to_all.42), channel_id=1, replica_groups=mesh['src'=16,'tgt'=16] {'tgt'}, dimensions={0} | all-to-all | bytes 720000 | tf_op jit(solution)/shard_map/all_to_all | solution.py:48
  124.5 0.2 reduce_sum.138
  124.7 0.2 broadcast_in_dim.22
  124.9 12.8 %all_to_all.59 = f32[16,1,5625]{2,1,0:T(1,128)S(1)} all-to-all(f32[16,1,5625]{2,1,0:T(1,128)S(1)} %broadcast_in_dim.22), channel_id=1, replica_groups=mesh['src'=16,'tgt'=16] {'src'}, dimensions={0} | all-to-all | bytes 720000 | tf_op jit(solution)/shard_map/all_to_all | solution.py:49
  137.6 0.2 reduce_sum.139
  137.9 0.2 broadcast_in_dim.23
  138.1 16.8 %all_to_all.60 = f32[16,1,5625]{2,1,0:T(1,128)S(1)} all-to-all(f32[16,1,5625]{2,1,0:T(1,128)S(1)} %broadcast_in_dim.23), channel_id=1, replica_groups=mesh['src'=16,'tgt'=16] {'tgt'}, dimensions={0} | all-to-all | bytes 720000 | tf_op jit(solution)/shard_map/all_to_all | solution.py:50
  154.8 0.8 reduce.8
  155.7 1.2 reshape_reshape.3
  (27 shorter events, 0.4 us)
Async XLA Ops:
  0.6 2.5 %copy-start = (bf16[300,2048]{1,0:T(8,128)(2,1)S(1)}, bf16[300,2048]{1,0:T(8,128)(2,1)}, u32[]{:S(2)}) copy-start(bf16[300,2048]{1,0:T(8,128)(2,1)} %param.6) | copy-start | bytes 3686404
  3.2 22.7 %copy-start.4 = (f32[1024]{0:T(1024)S(1)}, f32[1024]{0:T(1024)}, u32[]{:S(2)}) copy-start(f32[1024]{0:T(1024)} %param.8) | copy-start | bytes 12292
  25.9 18.0 %copy-start.2 = (f32[2048]{0:T(1024)S(1)}, f32[2048]{0:T(1024)}, u32[]{:S(2)}) copy-start(f32[2048]{0:T(1024)} %param.9) | copy-start | bytes 24580
  89.0 14.1 %copy-start.3 = (f32[1024]{0:T(1024)}, f32[1024]{0:T(1024)S(1)}, u32[]{:S(2)}) copy-start(f32[1024]{0:T(1024)S(1)} %add_subtract_fusion.3) | copy-start | bytes 12292
  103.2 1.7 %copy-start.5 = (f32[2048]{0:T(1024)}, f32[2048]{0:T(1024)S(1)}, u32[]{:S(2)}) copy-start(f32[2048]{0:T(1024)S(1)} %add_subtract_fusion) | copy-start | bytes 24580
  103.2 1.7 %copy-start.1 = (bf16[300,1024]{1,0:T(8,128)(2,1)S(1)}, bf16[300,1024]{1,0:T(8,128)(2,1)}, u32[]{:S(2)}) copy-start(bf16[300,1024]{1,0:T(8,128)(2,1)} %param.5) | copy-start | bytes 1843204

commit v4 on v3

--- a/solution.py
+++ b/solution.py
@@ -39,15 +39,15 @@
 
 
 def sum_all(c, scale):
-    n = lax.axis_size("tgt")
-    m = lax.axis_size("src")
+    n = lax.axis_size("src")
+    m = lax.axis_size("tgt")
     rows, cols = c.shape
     k = rows * cols
     per = -(-k // n)
     x = jnp.pad(c.reshape(-1), (0, per * n - k)).reshape(n, per)
-    x = jnp.sum(lax.all_to_all(x, "tgt", 0, 0, tiled=True), axis=0)
-    x = jnp.sum(lax.all_to_all(jnp.broadcast_to(x[None], (m, per)), "src", 0, 0, tiled=True), axis=0) * scale
-    x = lax.all_to_all(jnp.broadcast_to(x[None], (n, per)), "tgt", 0, 0, tiled=True)
+    x = jnp.sum(lax.all_to_all(x, "src", 0, 0, tiled=True), axis=0)
+    x = jnp.sum(lax.all_to_all(jnp.broadcast_to(x[None], (m, per)), "tgt", 0, 0, tiled=True), axis=0) * scale
+    x = lax.all_to_all(jnp.broadcast_to(x[None], (n, per)), "src", 0, 0, tiled=True)
     return x.reshape(-1)[:k].reshape(rows, cols)
 
 

time: 157 us -> 153 us (0.975)
  blocking collectives: 128 us -> 124 us
    all_to_all x3, blocking collectives: 47 us -> 42.6 us  [the longest x1 18.4 us: sum_all(): lax.all_to_all(jnp.broadcast_to(x[None], (m, per)), 'tgt', 0, 0, tiled=True)]
where the time goes in v4:
time: 153 us
  blocking collectives  124 us (81%)
  other arithmetic  16.6 us (11%)
  matrix products  7.83 us (5%)
  local copies, waits for them, and re-layouts  3 us (2%)
    all_to_all x6, blocking collectives, merge_lse(): got = lax.all_to_all(sent, axis, 0, 0, tiled=False)  81.5 us
    all_to_all x1, blocking collectives, sum_all(): lax.all_to_all(jnp.broadcast_to(x[None], (m, per)), 'tgt', 0, 0, tiled=True)  18.4 us
    all_to_all x1, blocking collectives, sum_all(): lax.all_to_all(jnp.broadcast_to(x[None], (n, per)), 'src', 0, 0, tiled=True)  12.7 us
    all_to_all x1, blocking collectives, sum_all(): x = jnp.sum(lax.all_to_all(x, 'src', 0, 0, tiled=True), axis=0)  11.5 us
    reduce_sum x3, other arithmetic, col_lse(): totals = jnp.sum(jnp.exp(shifted - peaks[None, :]), axis=0)  5.44 us
    reduce_sum x3, other arithmetic, row_lse(): totals = jnp.sum(jnp.exp(shifted - peaks[:, None]), axis=1)  5.14 us

profile of v4, /device:TPU:1, one launch (start us, length us, event | category | flops | bytes accessed | tf_op | source)
XLA Modules:
  0.0 152.6 jit_solution(5660768813583877523)
XLA Ops:
  0.6 0.0 copy-start
  0.6 2.5 %convolution_convert_fusion = bf16[300,1024]{1,0:T(8,128)(2,1)S(1)} fusion(f32[300,300]{1,0:T(8,128)} %param.7, bf16[300,1024]{1,0:T(8,128)(2,1)} %param.5), kind=kOutput, calls=%fused_computation.15 | convolution fusion | flops 1106227200 | bytes 1588800 | tf_op jit(solution)/shard_map/dot_general | solution.py:55
  3.2 2.5 %fusion.33 = (f32[1024]{0:T(1024)S(1)}, f32[1024,2048]{1,0:T(8,128)S(1)}) fusion(bf16[300,1024]{1,0:T(8,128)(2,1)S(1)} %convolution_convert_fusion, bf16[300,2048]{1,0:T(8,128)(2,1)S(1)} %copy-done), kind=kOutput, calls=%fused_computation.72 | convolution fusion | flops 1260387328 | bytes 10235904 | tf_op jit(solution)/shard_map/dot_general | solution.py:58
  5.7 1.3 exponential_reduce_fusion.5
  7.0 18.7 %all_to_all.52 = f32[16,2,1024]{2,1,0:T(2,128)S(1)} all-to-all(f32[16,2,1024]{2,1,0:T(2,128)S(1)} %broadcast_in_dim.16), channel_id=1, replica_groups=mesh['src'=16,'tgt'=16] {'tgt'}, dimensions={0} | all-to-all | bytes 262144 | tf_op jit(solution)/shard_map/all_to_all | solution.py:14
  25.7 0.1 fusion.32
  25.9 0.6 add_reduce_fusion.3
  26.5 1.8 %exponential_reduce_fusion.4 = f32[2048]{0:T(1024)S(1)} fusion(f32[1024,2048]{1,0:T(8,128)S(1)} %get-tuple-element.22, f32[2048]{0:T(1024)S(1)} %add_reduce_fusion.3, f32[1024]{0:T(1024)S(1)} %add_subtract_fusion.5), kind=kLoop, calls=%fused_computation.5 | loop fusion | flops 6289408 | bytes 8409088 | tf_op jit(solution)/shard_map/reduce_sum | solution.py:28
  28.4 0.1 broadcast_in_dim.17
  28.5 15.1 %all_to_all.53 = f32[16,2,2048]{2,1,0:T(2,128)S(1)} all-to-all(f32[16,2,2048]{2,1,0:T(2,128)S(1)} %broadcast_in_dim.17), channel_id=1, replica_groups=mesh['src'=16,'tgt'=16] {'src'}, dimensions={0} | all-to-all | bytes 524288 | tf_op jit(solution)/shard_map/all_to_all | solution.py:14
  43.6 0.2 fusion.29
  43.8 0.1 fusion.14
  43.9 0.6 add_reduce_fusion.2
  44.5 1.9 %exponential_reduce_fusion.3 = f32[1024]{0:T(1024)S(1)} fusion(f32[1024,2048]{1,0:T(8,128)S(1)} %get-tuple-element.22, f32[1024]{0:T(1024)S(1)} %add_reduce_fusion.2, f32[2048]{0:T(1024)S(1)} %add_subtract_fusion.2), kind=kLoop, calls=%fused_computation.4 | loop fusion | flops 6290432 | bytes 8404992 | tf_op jit(solution)/shard_map/reduce_sum | solution.py:22
  46.5 12.7 %all_to_all.54 = f32[16,2,1024]{2,1,0:T(2,128)S(1)} all-to-all(f32[16,2,1024]{2,1,0:T(2,128)S(1)} %broadcast_in_dim.18), channel_id=1, replica_groups=mesh['src'=16,'tgt'=16] {'tgt'}, dimensions={0} | all-to-all | bytes 262144 | tf_op jit(solution)/shard_map/all_to_all | solution.py:14
  59.2 0.1 fusion.31
  59.4 0.6 add_reduce_fusion.1
  60.0 1.8 %exponential_reduce_fusion.2 = f32[2048]{0:T(1024)S(1)} fusion(f32[1024,2048]{1,0:T(8,128)S(1)} %get-tuple-element.22, f32[2048]{0:T(1024)S(1)} %add_reduce_fusion.1, f32[1024]{0:T(1024)S(1)} %add_subtract_fusion.4), kind=kLoop, calls=%fused_computation.3 | loop fusion | flops 6289408 | bytes 8409088 | tf_op jit(solution)/shard_map/reduce_sum | solution.py:28
  61.9 0.1 broadcast_in_dim.19
  62.0 11.2 %all_to_all.55 = f32[16,2,2048]{2,1,0:T(2,128)S(1)} all-to-all(f32[16,2,2048]{2,1,0:T(2,128)S(1)} %broadcast_in_dim.19), channel_id=1, replica_groups=mesh['src'=16,'tgt'=16] {'src'}, dimensions={0} | all-to-all | bytes 524288 | tf_op jit(solution)/shard_map/all_to_all | solution.py:14
  73.2 0.2 fusion.28
  73.4 0.1 fusion.10
  73.5 0.6 add_reduce_fusion
  74.1 1.9 %exponential_reduce_fusion.1 = f32[1024]{0:T(1024)S(1)} fusion(f32[1024,2048]{1,0:T(8,128)S(1)} %get-tuple-element.22, f32[1024]{0:T(1024)S(1)} %add_reduce_fusion, f32[2048]{0:T(1024)S(1)} %add_subtract_fusion.1), kind=kLoop, calls=%fused_computation.2 | loop fusion | flops 6290432 | bytes 8404992 | tf_op jit(solution)/shard_map/reduce_sum | solution.py:22
  76.2 12.7 %all_to_all.56 = f32[16,2,1024]{2,1,0:T(2,128)S(1)} all-to-all(f32[16,2,1024]{2,1,0:T(2,128)S(1)} %broadcast_in_dim.20), channel_id=1, replica_groups=mesh['src'=16,'tgt'=16] {'tgt'}, dimensions={0} | all-to-all | bytes 262144 | tf_op jit(solution)/shard_map/all_to_all | solution.py:14
  88.8 0.1 fusion.30
  89.0 0.0 copy-start.3
  89.0 0.6 add_reduce_fusion.4
  89.7 1.8 %exponential_reduce_fusion = f32[2048]{0:T(1024)S(1)} fusion(f32[1024,2048]{1,0:T(8,128)S(1)} %get-tuple-element.22, f32[2048]{0:T(1024)S(1)} %add_reduce_fusion.4, f32[1024]{0:T(1024)S(1)} %add_subtract_fusion.3), kind=kLoop, calls=%fused_computation.1 | loop fusion | flops 6289408 | bytes 8409088 | tf_op jit(solution)/shard_map/reduce_sum | solution.py:28
  91.5 0.1 broadcast_in_dim.21
  91.6 11.2 %all_to_all.57 = f32[16,2,2048]{2,1,0:T(2,128)S(1)} all-to-all(f32[16,2,2048]{2,1,0:T(2,128)S(1)} %broadcast_in_dim.21), channel_id=1, replica_groups=mesh['src'=16,'tgt'=16] {'src'}, dimensions={0} | all-to-all | bytes 524288 | tf_op jit(solution)/shard_map/all_to_all | solution.py:14
  102.8 0.2 fusion.27
  103.0 0.1 fusion.6
  103.2 0.0 copy-start.5
  103.2 0.0 copy-start.1
  103.2 1.7 %fusion = f32[1024,300]{0,1:T(8,128)S(1)} fusion(bf16[300,2048]{1,0:T(8,128)(2,1)S(1)} %copy-done, f32[1024,2048]{1,0:T(8,128)S(1)} %get-tuple-element.22, f32[2048]{0:T(1024)S(1)} %add_subtract_fusion, f32[1024]{0:T(1024)S(1)} %add_subtract_fusion.3), kind=kOutput, calls=%fused_computation.12 | convolution fusion | flops 1264582656 | bytes 10858496 | tf_op jit(solution)/shard_map/dot_general | solution.py:68
  104.9 1.1 convolution_bitcast_fusion
  106.0 0.2 copy.37
  106.2 0.8 all_to_all.42
  107.0 11.5 %all_to_all.58 = f32[16,1,5625]{2,1,0:T(1,128)S(1)} all-to-all(f32[16,1,5625]{2,1,0:T(1,128)S(1)} %all_to_all.42), channel_id=1, replica_groups=mesh['src'=16,'tgt'=16] {'src'}, dimensions={0} | all-to-all | bytes 720000 | tf_op jit(solution)/shard_map/all_to_all | solution.py:48
  118.5 0.2 reduce_sum.138
  118.7 0.2 broadcast_in_dim.22
  118.9 18.4 %all_to_all.59 = f32[16,1,5625]{2,1,0:T(1,128)S(1)} all-to-all(f32[16,1,5625]{2,1,0:T(1,128)S(1)} %broadcast_in_dim.22), channel_id=1, replica_groups=mesh['src'=16,'tgt'=16] {'tgt'}, dimensions={0} | all-to-all | bytes 720000 | tf_op jit(solution)/shard_map/all_to_all | solution.py:49
  137.3 0.2 reduce_sum.139
  137.6 0.2 broadcast_in_dim.23
  137.8 12.7 %all_to_all.60 = f32[16,1,5625]{2,1,0:T(1,128)S(1)} all-to-all(f32[16,1,5625]{2,1,0:T(1,128)S(1)} %broadcast_in_dim.23), channel_id=1, replica_groups=mesh['src'=16,'tgt'=16] {'src'}, dimensions={0} | all-to-all | bytes 720000 | tf_op jit(solution)/shard_map/all_to_all | solution.py:50
  150.5 0.8 reduce.8
  151.4 1.2 reshape_reshape.3
  (27 shorter events, 0.4 us)
Async XLA Ops:
  0.6 2.5 %copy-start = (bf16[300,2048]{1,0:T(8,128)(2,1)S(1)}, bf16[300,2048]{1,0:T(8,128)(2,1)}, u32[]{:S(2)}) copy-start(bf16[300,2048]{1,0:T(8,128)(2,1)} %param.6) | copy-start | bytes 3686404
  3.2 22.7 %copy-start.4 = (f32[1024]{0:T(1024)S(1)}, f32[1024]{0:T(1024)}, u32[]{:S(2)}) copy-start(f32[1024]{0:T(1024)} %param.8) | copy-start | bytes 12292
  25.9 18.0 %copy-start.2 = (f32[2048]{0:T(1024)S(1)}, f32[2048]{0:T(1024)}, u32[]{:S(2)}) copy-start(f32[2048]{0:T(1024)} %param.9) | copy-start | bytes 24580
  89.0 14.1 %copy-start.3 = (f32[1024]{0:T(1024)}, f32[1024]{0:T(1024)S(1)}, u32[]{:S(2)}) copy-start(f32[1024]{0:T(1024)S(1)} %add_subtract_fusion.3) | copy-start | bytes 12292
  103.2 1.7 %copy-start.5 = (f32[2048]{0:T(1024)}, f32[2048]{0:T(1024)S(1)}, u32[]{:S(2)}) copy-start(f32[2048]{0:T(1024)S(1)} %add_subtract_fusion) | copy-start | bytes 24580
  103.2 1.7 %copy-start.1 = (bf16[300,1024]{1,0:T(8,128)(2,1)S(1)}, bf16[300,1024]{1,0:T(8,128)(2,1)}, u32[]{:S(2)}) copy-start(bf16[300,1024]{1,0:T(8,128)(2,1)} %param.5) | copy-start | bytes 1843204

commit v5 on v4

--- a/solution.py
+++ b/solution.py
@@ -1,10 +1,12 @@
 import jax
 import jax.numpy as jnp
 from jax import lax
-from jax.sharding import PartitionSpec as P
+from jax.sharding import Mesh, PartitionSpec as P
 
 D = 300
 ITERS = 3
+TGT = ("tz", "tc")
+WIDE = ("src", "tc")
 
 
 def merge_lse(peaks, totals, axis):
@@ -20,7 +22,7 @@
 def row_lse(shifted):
     peaks = jnp.max(shifted, axis=1)
     totals = jnp.sum(jnp.exp(shifted - peaks[:, None]), axis=1)
-    return merge_lse(peaks, totals, "tgt")
+    return merge_lse(peaks, totals, TGT)
 
 
 def col_lse(shifted):
@@ -39,15 +41,15 @@
 
 
 def sum_all(c, scale):
-    n = lax.axis_size("src")
-    m = lax.axis_size("tgt")
+    n = lax.axis_size(WIDE)
+    m = lax.axis_size("tz")
     rows, cols = c.shape
     k = rows * cols
     per = -(-k // n)
     x = jnp.pad(c.reshape(-1), (0, per * n - k)).reshape(n, per)
-    x = jnp.sum(lax.all_to_all(x, "src", 0, 0, tiled=True), axis=0)
-    x = jnp.sum(lax.all_to_all(jnp.broadcast_to(x[None], (m, per)), "tgt", 0, 0, tiled=True), axis=0) * scale
-    x = lax.all_to_all(jnp.broadcast_to(x[None], (n, per)), "src", 0, 0, tiled=True)
+    x = jnp.sum(lax.all_to_all(x, WIDE, 0, 0, tiled=True), axis=0)
+    x = jnp.sum(lax.all_to_all(jnp.broadcast_to(x[None], (m, per)), "tz", 0, 0, tiled=True), axis=0) * scale
+    x = lax.all_to_all(jnp.broadcast_to(x[None], (n, per)), WIDE, 0, 0, tiled=True)
     return x.reshape(-1)[:k].reshape(rows, cols)
 
 
@@ -74,7 +76,9 @@
 
 
 def solution(mesh):
-    placed = (P(None, "src"), P(None, "tgt"), P(), P("src"), P("tgt"))
+    n_src, n_tgt = mesh.devices.shape
+    fine = Mesh(mesh.devices.reshape(n_src, n_tgt // 2, 2), ("src",) + TGT)
+    placed = (P(None, "src"), P(None, TGT), P(), P("src"), P(TGT))
     return jax.shard_map(
-        per_device, mesh=mesh, in_specs=placed, out_specs=(P("src"), P("tgt"), P()), check_vma=False
+        per_device, mesh=fine, in_specs=placed, out_specs=(P("src"), P(TGT), P()), check_vma=False
     )

time: 153 us -> 149 us (0.974)
  blocking collectives: 124 us -> 120 us
    all_to_all x3, blocking collectives: 42.6 us -> 38.6 us  [the longest x1 14.7 us: sum_all(): lax.all_to_all(jnp.broadcast_to(x[None], (n, per)), WIDE, 0, 0, tiled=True)]
    reshape x0 -> x3, local copies, waits for them, and re-layouts: none -> 1.89 us  [the longest x2 1.44 us: sum_all(): return x.reshape(-1)[:k].reshape(rows, cols)]
where the time goes in v5:
time: 149 us
  blocking collectives  120 us (81%)
  other arithmetic  16.5 us (11%)
  matrix products  7.83 us (5%)
  local copies, waits for them, and re-layouts  3.29 us (2%)
    all_to_all x6, blocking collectives, merge_lse(): got = lax.all_to_all(sent, axis, 0, 0, tiled=False)  81.5 us
    all_to_all x1, blocking collectives, sum_all(): lax.all_to_all(jnp.broadcast_to(x[None], (n, per)), WIDE, 0, 0, tiled=True)  14.7 us
    all_to_all x1, blocking collectives, sum_all(): x = jnp.sum(lax.all_to_all(x, WIDE, 0, 0, tiled=True), axis=0)  13.9 us
    all_to_all x1, blocking collectives, sum_all(): lax.all_to_all(jnp.broadcast_to(x[None], (m, per)), 'tz', 0, 0, tiled=True)  10 us
    reduce_sum x3, other arithmetic, col_lse(): totals = jnp.sum(jnp.exp(shifted - peaks[None, :]), axis=0)  5.44 us
    reduce_sum x3, other arithmetic, row_lse(): totals = jnp.sum(jnp.exp(shifted - peaks[:, None]), axis=1)  5.14 us

profile of v5, /device:TPU:1, one launch (start us, length us, event | category | flops | bytes accessed | tf_op | source)
XLA Modules:
  0.0 148.7 jit_solution(11986919490906532270)
XLA Ops:
  0.6 0.0 copy-start
  0.6 2.5 %convolution_convert_fusion = bf16[300,1024]{1,0:T(8,128)(2,1)S(1)} fusion(f32[300,300]{1,0:T(8,128)} %param.7, bf16[300,1024]{1,0:T(8,128)(2,1)} %param.5), kind=kOutput, calls=%fused_computation.15 | convolution fusion | flops 1106227200 | bytes 1588800 | tf_op jit(solution)/shard_map/dot_general | solution.py:57
  3.2 2.5 %fusion.33 = (f32[1024]{0:T(1024)S(1)}, f32[1024,2048]{1,0:T(8,128)S(1)}) fusion(bf16[300,1024]{1,0:T(8,128)(2,1)S(1)} %convolution_convert_fusion, bf16[300,2048]{1,0:T(8,128)(2,1)S(1)} %copy-done), kind=kOutput, calls=%fused_computation.72 | convolution fusion | flops 1260387328 | bytes 10235904 | tf_op jit(solution)/shard_map/dot_general | solution.py:60
  5.7 1.3 exponential_reduce_fusion.5
  7.0 18.7 %all_to_all.51 = f32[16,2,1024]{2,1,0:T(2,128)S(1)} all-to-all(f32[16,2,1024]{2,1,0:T(2,128)S(1)} %broadcast_in_dim.16), channel_id=1, replica_groups=mesh['src'=16,'tz'=8,'tc'=2] {'tz','tc'}, dimensions={0} | all-to-all | bytes 262144 | tf_op jit(solution)/shard_map/all_to_all | solution.py:16
  25.7 0.1 fusion.32
  25.9 0.6 add_reduce_fusion.3
  26.5 1.8 %exponential_reduce_fusion.4 = f32[2048]{0:T(1024)S(1)} fusion(f32[1024,2048]{1,0:T(8,128)S(1)} %get-tuple-element.22, f32[2048]{0:T(1024)S(1)} %add_reduce_fusion.3, f32[1024]{0:T(1024)S(1)} %add_subtract_fusion.5), kind=kLoop, calls=%fused_computation.5 | loop fusion | flops 6289408 | bytes 8409088 | tf_op jit(solution)/shard_map/reduce_sum | solution.py:30
  28.4 0.1 broadcast_in_dim.17
  28.5 15.1 %all_to_all.52 = f32[16,2,2048]{2,1,0:T(2,128)S(1)} all-to-all(f32[16,2,2048]{2,1,0:T(2,128)S(1)} %broadcast_in_dim.17), channel_id=1, replica_groups=mesh['src'=16,'tz'=8,'tc'=2] {'src'}, dimensions={0} | all-to-all | bytes 524288 | tf_op jit(solution)/shard_map/all_to_all | solution.py:16
  43.6 0.2 fusion.29
  43.8 0.1 fusion.14
  43.9 0.6 add_reduce_fusion.2
  44.5 1.9 %exponential_reduce_fusion.3 = f32[1024]{0:T(1024)S(1)} fusion(f32[1024,2048]{1,0:T(8,128)S(1)} %get-tuple-element.22, f32[1024]{0:T(1024)S(1)} %add_reduce_fusion.2, f32[2048]{0:T(1024)S(1)} %add_subtract_fusion.2), kind=kLoop, calls=%fused_computation.4 | loop fusion | flops 6290432 | bytes 8404992 | tf_op jit(solution)/shard_map/reduce_sum | solution.py:24
  46.5 12.7 %all_to_all.53 = f32[16,2,1024]{2,1,0:T(2,128)S(1)} all-to-all(f32[16,2,1024]{2,1,0:T(2,128)S(1)} %broadcast_in_dim.18), channel_id=1, replica_groups=mesh['src'=16,'tz'=8,'tc'=2] {'tz','tc'}, dimensions={0} | all-to-all | bytes 262144 | tf_op jit(solution)/shard_map/all_to_all | solution.py:16
  59.2 0.1 fusion.31
  59.4 0.6 add_reduce_fusion.1
  60.0 1.8 %exponential_reduce_fusion.2 = f32[2048]{0:T(1024)S(1)} fusion(f32[1024,2048]{1,0:T(8,128)S(1)} %get-tuple-element.22, f32[2048]{0:T(1024)S(1)} %add_reduce_fusion.1, f32[1024]{0:T(1024)S(1)} %add_subtract_fusion.4), kind=kLoop, calls=%fused_computation.3 | loop fusion | flops 6289408 | bytes 8409088 | tf_op jit(solution)/shard_map/reduce_sum | solution.py:30
  61.9 0.1 broadcast_in_dim.19
  62.0 11.2 %all_to_all.54 = f32[16,2,2048]{2,1,0:T(2,128)S(1)} all-to-all(f32[16,2,2048]{2,1,0:T(2,128)S(1)} %broadcast_in_dim.19), channel_id=1, replica_groups=mesh['src'=16,'tz'=8,'tc'=2] {'src'}, dimensions={0} | all-to-all | bytes 524288 | tf_op jit(solution)/shard_map/all_to_all | solution.py:16
  73.2 0.2 fusion.28
  73.4 0.1 fusion.10
  73.5 0.6 add_reduce_fusion
  74.1 1.9 %exponential_reduce_fusion.1 = f32[1024]{0:T(1024)S(1)} fusion(f32[1024,2048]{1,0:T(8,128)S(1)} %get-tuple-element.22, f32[1024]{0:T(1024)S(1)} %add_reduce_fusion, f32[2048]{0:T(1024)S(1)} %add_subtract_fusion.1), kind=kLoop, calls=%fused_computation.2 | loop fusion | flops 6290432 | bytes 8404992 | tf_op jit(solution)/shard_map/reduce_sum | solution.py:24
  76.2 12.7 %all_to_all.55 = f32[16,2,1024]{2,1,0:T(2,128)S(1)} all-to-all(f32[16,2,1024]{2,1,0:T(2,128)S(1)} %broadcast_in_dim.20), channel_id=1, replica_groups=mesh['src'=16,'tz'=8,'tc'=2] {'tz','tc'}, dimensions={0} | all-to-all | bytes 262144 | tf_op jit(solution)/shard_map/all_to_all | solution.py:16
  88.8 0.1 fusion.30
  89.0 0.0 copy-start.3
  89.0 0.6 add_reduce_fusion.4
  89.7 1.8 %exponential_reduce_fusion = f32[2048]{0:T(1024)S(1)} fusion(f32[1024,2048]{1,0:T(8,128)S(1)} %get-tuple-element.22, f32[2048]{0:T(1024)S(1)} %add_reduce_fusion.4, f32[1024]{0:T(1024)S(1)} %add_subtract_fusion.3), kind=kLoop, calls=%fused_computation.1 | loop fusion | flops 6289408 | bytes 8409088 | tf_op jit(solution)/shard_map/reduce_sum | solution.py:30
  91.5 0.1 broadcast_in_dim.21
  91.6 11.2 %all_to_all.56 = f32[16,2,2048]{2,1,0:T(2,128)S(1)} all-to-all(f32[16,2,2048]{2,1,0:T(2,128)S(1)} %broadcast_in_dim.21), channel_id=1, replica_groups=mesh['src'=16,'tz'=8,'tc'=2] {'src'}, dimensions={0} | all-to-all | bytes 524288 | tf_op jit(solution)/shard_map/all_to_all | solution.py:16
  102.8 0.2 fusion.27
  103.0 0.1 fusion.6
  103.2 0.0 copy-start.5
  103.2 1.7 %fusion = f32[1024,300]{0,1:T(8,128)S(1)} fusion(bf16[300,2048]{1,0:T(8,128)(2,1)S(1)} %copy-done, f32[1024,2048]{1,0:T(8,128)S(1)} %get-tuple-element.22, f32[2048]{0:T(1024)S(1)} %add_subtract_fusion, f32[1024]{0:T(1024)S(1)} %add_subtract_fusion.3), kind=kOutput, calls=%fused_computation.12 | convolution fusion | flops 1264582656 | bytes 10858496 | tf_op jit(solution)/shard_map/dot_general | solution.py:70
  104.9 1.1 convolution_bitcast_fusion
  106.0 0.2 copy.28
  106.2 0.5 reshape.59
  106.7 0.5 all_to_all.38
  107.2 13.9 %all_to_all.57 = f32[32,1,2813]{2,1,0:T(1,128)S(1)} all-to-all(f32[32,1,2813]{2,1,0:T(1,128)S(1)} %all_to_all.38), channel_id=1, replica_groups=mesh['src'=16,'tz'=8,'tc'=2] {'src','tc'}, dimensions={0} | all-to-all | bytes 720128 | tf_op jit(solution)/shard_map/all_to_all | solution.py:50
  121.1 0.2 reduce_sum.138
  121.4 10.0 %all_to_all.58 = f32[8,1,2813]{2,1,0:T(1,128)S(1)} all-to-all(f32[8,1,2813]{2,1,0:T(1,128)S(1)} %broadcast_in_dim.22), channel_id=1, replica_groups=mesh['src'=16,'tz'=8,'tc'=2] {'tz'}, dimensions={0} | all-to-all | bytes 180032 | tf_op jit(solution)/shard_map/all_to_all | solution.py:51
  131.4 0.1 reduce_sum.139
  131.5 0.2 broadcast_in_dim.23
  131.7 14.7 %all_to_all.59 = f32[32,1,2813]{2,1,0:T(1,128)S(1)} all-to-all(f32[32,1,2813]{2,1,0:T(1,128)S(1)} %broadcast_in_dim.23), channel_id=1, replica_groups=mesh['src'=16,'tz'=8,'tc'=2] {'src','tc'}, dimensions={0} | all-to-all | bytes 720128 | tf_op jit(solution)/shard_map/all_to_all | solution.py:52
  146.4 0.8 reduce.8
  147.2 0.2 reshape.60
  147.4 1.2 reshape.61
  (30 shorter events, 0.5 us)
Async XLA Ops:
  0.6 2.5 %copy-start = (bf16[300,2048]{1,0:T(8,128)(2,1)S(1)}, bf16[300,2048]{1,0:T(8,128)(2,1)}, u32[]{:S(2)}) copy-start(bf16[300,2048]{1,0:T(8,128)(2,1)} %param.6) | copy-start | bytes 3686404
  3.2 22.7 %copy-start.4 = (f32[1024]{0:T(1024)S(1)}, f32[1024]{0:T(1024)}, u32[]{:S(2)}) copy-start(f32[1024]{0:T(1024)} %param.8) | copy-start | bytes 12292
  25.9 18.0 %copy-start.2 = (f32[2048]{0:T(1024)S(1)}, f32[2048]{0:T(1024)}, u32[]{:S(2)}) copy-start(f32[2048]{0:T(1024)} %param.9) | copy-start | bytes 24580
  89.0 14.1 %copy-start.3 = (f32[1024]{0:T(1024)}, f32[1024]{0:T(1024)S(1)}, u32[]{:S(2)}) copy-start(f32[1024]{0:T(1024)S(1)} %add_subtract_fusion.3) | copy-start | bytes 12292
  103.2 1.7 %copy-start.5 = (f32[2048]{0:T(1024)}, f32[2048]{0:T(1024)S(1)}, u32[]{:S(2)}) copy-start(f32[2048]{0:T(1024)S(1)} %add_subtract_fusion) | copy-start | bytes 24580
  103.2 1.7 %copy-start.1 = (bf16[300,1024]{1,0:T(8,128)(2,1)S(1)}, bf16[300,1024]{1,0:T(8,128)(2,1)}, u32[]{:S(2)}) copy-start(bf16[300,1024]{1,0:T(8,128)(2,1)} %param.5) | copy-start | bytes 1843204

commit v6 on v5

--- a/solution.py
+++ b/solution.py
@@ -22,7 +22,7 @@
 def row_lse(shifted):
     peaks = jnp.max(shifted, axis=1)
     totals = jnp.sum(jnp.exp(shifted - peaks[:, None]), axis=1)
-    return merge_lse(peaks, totals, TGT)
+    return merge_lse(peaks, totals, ("tc", "tz"))
 
 
 def col_lse(shifted):

time: 149 us -> 147 us (0.987)
  blocking collectives: 120 us -> 118 us
    all_to_all x6, blocking collectives: 81.5 us -> 77.6 us  [merge_lse(): got = lax.all_to_all(sent, axis, 0, 0, tiled=False)]
    all_to_all x1, blocking collectives: 13.9 us -> 15.5 us  [sum_all(): x = jnp.sum(lax.all_to_all(x, WIDE, 0, 0, tiled=True), axis=0)]
where the time goes in v6:
time: 147 us
  blocking collectives  118 us (80%)
  other arithmetic  16.5 us (11%)
  matrix products  7.83 us (5%)
  local copies, waits for them, and re-layouts  3.29 us (2%)
    all_to_all x6, blocking collectives, merge_lse(): got = lax.all_to_all(sent, axis, 0, 0, tiled=False)  77.6 us
    all_to_all x1, blocking collectives, sum_all(): x = jnp.sum(lax.all_to_all(x, WIDE, 0, 0, tiled=True), axis=0)  15.5 us
    all_to_all x1, blocking collectives, sum_all(): lax.all_to_all(jnp.broadcast_to(x[None], (n, per)), WIDE, 0, 0, tiled=True)  14.9 us
    all_to_all x1, blocking collectives, sum_all(): lax.all_to_all(jnp.broadcast_to(x[None], (m, per)), 'tz', 0, 0, tiled=True)  10 us
    reduce_sum x3, other arithmetic, col_lse(): totals = jnp.sum(jnp.exp(shifted - peaks[None, :]), axis=0)  5.44 us
    reduce_sum x3, other arithmetic, row_lse(): totals = jnp.sum(jnp.exp(shifted - peaks[:, None]), axis=1)  5.14 us

profile of v6, /device:TPU:1, one launch (start us, length us, event | category | flops | bytes accessed | tf_op | source)
XLA Modules:
  0.0 146.6 jit_solution(14682600084408471802)
XLA Ops:
  0.6 0.0 copy-start
  0.6 2.5 %convolution_convert_fusion = bf16[300,1024]{1,0:T(8,128)(2,1)S(1)} fusion(f32[300,300]{1,0:T(8,128)} %param.7, bf16[300,1024]{1,0:T(8,128)(2,1)} %param.5), kind=kOutput, calls=%fused_computation.15 | convolution fusion | flops 1106227200 | bytes 1588800 | tf_op jit(solution)/shard_map/dot_general | solution.py:57
  3.2 2.5 %fusion.33 = (f32[1024]{0:T(1024)S(1)}, f32[1024,2048]{1,0:T(8,128)S(1)}) fusion(bf16[300,1024]{1,0:T(8,128)(2,1)S(1)} %convolution_convert_fusion, bf16[300,2048]{1,0:T(8,128)(2,1)S(1)} %copy-done), kind=kOutput, calls=%fused_computation.72 | convolution fusion | flops 1260387328 | bytes 10235904 | tf_op jit(solution)/shard_map/dot_general | solution.py:60
  5.7 1.3 exponential_reduce_fusion.5
  7.0 17.1 %all_to_all.51 = f32[16,2,1024]{2,1,0:T(2,128)S(1)} all-to-all(f32[16,2,1024]{2,1,0:T(2,128)S(1)} %broadcast_in_dim.16), channel_id=1, replica_groups=mesh['src'=16,'tz'=8,'tc'=2] {'tc','tz'}, dimensions={0} | all-to-all | bytes 262144 | tf_op jit(solution)/shard_map/all_to_all | solution.py:16
  24.2 0.1 fusion.32
  24.4 0.6 add_reduce_fusion.3
  25.0 1.8 %exponential_reduce_fusion.4 = f32[2048]{0:T(1024)S(1)} fusion(f32[1024,2048]{1,0:T(8,128)S(1)} %get-tuple-element.22, f32[2048]{0:T(1024)S(1)} %add_reduce_fusion.3, f32[1024]{0:T(1024)S(1)} %add_subtract_fusion.5), kind=kLoop, calls=%fused_computation.5 | loop fusion | flops 6289408 | bytes 8409088 | tf_op jit(solution)/shard_map/reduce_sum | solution.py:30
  26.9 0.1 broadcast_in_dim.17
  27.0 14.1 %all_to_all.52 = f32[16,2,2048]{2,1,0:T(2,128)S(1)} all-to-all(f32[16,2,2048]{2,1,0:T(2,128)S(1)} %broadcast_in_dim.17), channel_id=1, replica_groups=mesh['src'=16,'tz'=8,'tc'=2] {'src'}, dimensions={0} | all-to-all | bytes 524288 | tf_op jit(solution)/shard_map/all_to_all | solution.py:16
  41.1 0.2 fusion.29
  41.3 0.1 fusion.14
  41.4 0.6 add_reduce_fusion.2
  42.0 1.9 %exponential_reduce_fusion.3 = f32[1024]{0:T(1024)S(1)} fusion(f32[1024,2048]{1,0:T(8,128)S(1)} %get-tuple-element.22, f32[1024]{0:T(1024)S(1)} %add_reduce_fusion.2, f32[2048]{0:T(1024)S(1)} %add_subtract_fusion.2), kind=kLoop, calls=%fused_computation.4 | loop fusion | flops 6290432 | bytes 8404992 | tf_op jit(solution)/shard_map/reduce_sum | solution.py:24
  44.0 13.0 %all_to_all.53 = f32[16,2,1024]{2,1,0:T(2,128)S(1)} all-to-all(f32[16,2,1024]{2,1,0:T(2,128)S(1)} %broadcast_in_dim.18), channel_id=1, replica_groups=mesh['src'=16,'tz'=8,'tc'=2] {'tc','tz'}, dimensions={0} | all-to-all | bytes 262144 | tf_op jit(solution)/shard_map/all_to_all | solution.py:16
  57.0 0.1 fusion.31
  57.2 0.6 add_reduce_fusion.1
  57.9 1.8 %exponential_reduce_fusion.2 = f32[2048]{0:T(1024)S(1)} fusion(f32[1024,2048]{1,0:T(8,128)S(1)} %get-tuple-element.22, f32[2048]{0:T(1024)S(1)} %add_reduce_fusion.1, f32[1024]{0:T(1024)S(1)} %add_subtract_fusion.4), kind=kLoop, calls=%fused_computation.3 | loop fusion | flops 6289408 | bytes 8409088 | tf_op jit(solution)/shard_map/reduce_sum | solution.py:30
  59.7 0.1 broadcast_in_dim.19
  59.8 10.2 %all_to_all.54 = f32[16,2,2048]{2,1,0:T(2,128)S(1)} all-to-all(f32[16,2,2048]{2,1,0:T(2,128)S(1)} %broadcast_in_dim.19), channel_id=1, replica_groups=mesh['src'=16,'tz'=8,'tc'=2] {'src'}, dimensions={0} | all-to-all | bytes 524288 | tf_op jit(solution)/shard_map/all_to_all | solution.py:16
  70.0 0.2 fusion.28
  70.2 0.1 fusion.10
  70.3 0.6 add_reduce_fusion
  70.9 1.9 %exponential_reduce_fusion.1 = f32[1024]{0:T(1024)S(1)} fusion(f32[1024,2048]{1,0:T(8,128)S(1)} %get-tuple-element.22, f32[1024]{0:T(1024)S(1)} %add_reduce_fusion, f32[2048]{0:T(1024)S(1)} %add_subtract_fusion.1), kind=kLoop, calls=%fused_computation.2 | loop fusion | flops 6290432 | bytes 8404992 | tf_op jit(solution)/shard_map/reduce_sum | solution.py:24
  73.0 13.0 %all_to_all.55 = f32[16,2,1024]{2,1,0:T(2,128)S(1)} all-to-all(f32[16,2,1024]{2,1,0:T(2,128)S(1)} %broadcast_in_dim.20), channel_id=1, replica_groups=mesh['src'=16,'tz'=8,'tc'=2] {'tc','tz'}, dimensions={0} | all-to-all | bytes 262144 | tf_op jit(solution)/shard_map/all_to_all | solution.py:16
  85.9 0.1 fusion.30
  86.1 0.0 copy-start.3
  86.1 0.6 add_reduce_fusion.4
  86.8 1.8 %exponential_reduce_fusion = f32[2048]{0:T(1024)S(1)} fusion(f32[1024,2048]{1,0:T(8,128)S(1)} %get-tuple-element.22, f32[2048]{0:T(1024)S(1)} %add_reduce_fusion.4, f32[1024]{0:T(1024)S(1)} %add_subtract_fusion.3), kind=kLoop, calls=%fused_computation.1 | loop fusion | flops 6289408 | bytes 8409088 | tf_op jit(solution)/shard_map/reduce_sum | solution.py:30
  88.6 0.1 broadcast_in_dim.21
  88.7 10.2 %all_to_all.56 = f32[16,2,2048]{2,1,0:T(2,128)S(1)} all-to-all(f32[16,2,2048]{2,1,0:T(2,128)S(1)} %broadcast_in_dim.21), channel_id=1, replica_groups=mesh['src'=16,'tz'=8,'tc'=2] {'src'}, dimensions={0} | all-to-all | bytes 524288 | tf_op jit(solution)/shard_map/all_to_all | solution.py:16
  98.9 0.2 fusion.27
  99.1 0.1 fusion.6
  99.3 0.0 copy-start.5
  99.3 1.7 %fusion = f32[1024,300]{0,1:T(8,128)S(1)} fusion(bf16[300,2048]{1,0:T(8,128)(2,1)S(1)} %copy-done, f32[1024,2048]{1,0:T(8,128)S(1)} %get-tuple-element.22, f32[2048]{0:T(1024)S(1)} %add_subtract_fusion, f32[1024]{0:T(1024)S(1)} %add_subtract_fusion.3), kind=kOutput, calls=%fused_computation.12 | convolution fusion | flops 1264582656 | bytes 10858496 | tf_op jit(solution)/shard_map/dot_general | solution.py:70
  101.0 1.1 convolution_bitcast_fusion
  102.1 0.2 copy.28
  102.3 0.5 reshape.59
  102.8 0.5 all_to_all.38
  103.3 15.5 %all_to_all.57 = f32[32,1,2813]{2,1,0:T(1,128)S(1)} all-to-all(f32[32,1,2813]{2,1,0:T(1,128)S(1)} %all_to_all.38), channel_id=1, replica_groups=mesh['src'=16,'tz'=8,'tc'=2] {'src','tc'}, dimensions={0} | all-to-all | bytes 720128 | tf_op jit(solution)/shard_map/all_to_all | solution.py:50
  118.8 0.2 reduce_sum.138
  119.1 10.0 %all_to_all.58 = f32[8,1,2813]{2,1,0:T(1,128)S(1)} all-to-all(f32[8,1,2813]{2,1,0:T(1,128)S(1)} %broadcast_in_dim.22), channel_id=1, replica_groups=mesh['src'=16,'tz'=8,'tc'=2] {'tz'}, dimensions={0} | all-to-all | bytes 180032 | tf_op jit(solution)/shard_map/all_to_all | solution.py:51
  129.1 0.1 reduce_sum.139
  129.2 0.2 broadcast_in_dim.23
  129.4 14.9 %all_to_all.59 = f32[32,1,2813]{2,1,0:T(1,128)S(1)} all-to-all(f32[32,1,2813]{2,1,0:T(1,128)S(1)} %broadcast_in_dim.23), channel_id=1, replica_groups=mesh['src'=16,'tz'=8,'tc'=2] {'src','tc'}, dimensions={0} | all-to-all | bytes 720128 | tf_op jit(solution)/shard_map/all_to_all | solution.py:52
  144.3 0.8 reduce.8
  145.2 0.2 reshape.60
  145.4 1.2 reshape.61
  (30 shorter events, 0.5 us)
Async XLA Ops:
  0.6 2.5 %copy-start = (bf16[300,2048]{1,0:T(8,128)(2,1)S(1)}, bf16[300,2048]{1,0:T(8,128)(2,1)}, u32[]{:S(2)}) copy-start(bf16[300,2048]{1,0:T(8,128)(2,1)} %param.6) | copy-start | bytes 3686404
  3.2 21.2 %copy-start.4 = (f32[1024]{0:T(1024)S(1)}, f32[1024]{0:T(1024)}, u32[]{:S(2)}) copy-start(f32[1024]{0:T(1024)} %param.8) | copy-start | bytes 12292
  24.4 17.0 %copy-start.2 = (f32[2048]{0:T(1024)S(1)}, f32[2048]{0:T(1024)}, u32[]{:S(2)}) copy-start(f32[2048]{0:T(1024)} %param.9) | copy-start | bytes 24580
  86.1 13.1 %copy-start.3 = (f32[1024]{0:T(1024)}, f32[1024]{0:T(1024)S(1)}, u32[]{:S(2)}) copy-start(f32[1024]{0:T(1024)S(1)} %add_subtract_fusion.3) | copy-start | bytes 12292
  99.3 1.7 %copy-start.5 = (f32[2048]{0:T(1024)}, f32[2048]{0:T(1024)S(1)}, u32[]{:S(2)}) copy-start(f32[2048]{0:T(1024)S(1)} %add_subtract_fusion) | copy-start | bytes 24580
  99.3 1.7 %copy-start.1 = (bf16[300,1024]{1,0:T(8,128)(2,1)S(1)}, bf16[300,1024]{1,0:T(8,128)(2,1)}, u32[]{:S(2)}) copy-start(bf16[300,1024]{1,0:T(8,128)(2,1)} %param.5) | copy-start | bytes 1843204

commit v7 on v6

--- a/solution.py
+++ b/solution.py
@@ -5,8 +5,9 @@
 
 D = 300
 ITERS = 3
-TGT = ("tz", "tc")
-WIDE = ("src", "tc")
+TGT = ("tzh", "tzl", "tc")
+Z = ("tzl", "tzh")
+WIDE = ("tc", "src")
 
 
 def merge_lse(peaks, totals, axis):
@@ -22,7 +23,7 @@
 def row_lse(shifted):
     peaks = jnp.max(shifted, axis=1)
     totals = jnp.sum(jnp.exp(shifted - peaks[:, None]), axis=1)
-    return merge_lse(peaks, totals, ("tc", "tz"))
+    return merge_lse(peaks, totals, ("tc", "tzh", "tzl"))
 
 
 def col_lse(shifted):
@@ -42,13 +43,13 @@
 
 def sum_all(c, scale):
     n = lax.axis_size(WIDE)
-    m = lax.axis_size("tz")
+    m = lax.axis_size(Z)
     rows, cols = c.shape
     k = rows * cols
     per = -(-k // n)
     x = jnp.pad(c.reshape(-1), (0, per * n - k)).reshape(n, per)
     x = jnp.sum(lax.all_to_all(x, WIDE, 0, 0, tiled=True), axis=0)
-    x = jnp.sum(lax.all_to_all(jnp.broadcast_to(x[None], (m, per)), "tz", 0, 0, tiled=True), axis=0) * scale
+    x = jnp.sum(lax.all_to_all(jnp.broadcast_to(x[None], (m, per)), Z, 0, 0, tiled=True), axis=0) * scale
     x = lax.all_to_all(jnp.broadcast_to(x[None], (n, per)), WIDE, 0, 0, tiled=True)
     return x.reshape(-1)[:k].reshape(rows, cols)
 
@@ -77,7 +78,7 @@
 
 def solution(mesh):
     n_src, n_tgt = mesh.devices.shape
-    fine = Mesh(mesh.devices.reshape(n_src, n_tgt // 2, 2), ("src",) + TGT)
+    fine = Mesh(mesh.devices.reshape(n_src, n_tgt // 4, 2, 2), ("src",) + TGT)
     placed = (P(None, "src"), P(None, TGT), P(), P("src"), P(TGT))
     return jax.shard_map(
         per_device, mesh=fine, in_specs=placed, out_specs=(P("src"), P(TGT), P()), check_vma=False

time: 147 us -> 145 us (0.986)
  blocking collectives: 118 us -> 116 us
where the time goes in v7:
time: 145 us
  blocking collectives  116 us (80%)
  other arithmetic  16.5 us (11%)
  matrix products  7.83 us (5%)
  local copies, waits for them, and re-layouts  3.29 us (2%)
    all_to_all x6, blocking collectives, merge_lse(): got = lax.all_to_all(sent, axis, 0, 0, tiled=False)  77.6 us
    all_to_all x1, blocking collectives, sum_all(): x = jnp.sum(lax.all_to_all(x, WIDE, 0, 0, tiled=True), axis=0)  14.8 us
    all_to_all x1, blocking collectives, sum_all(): lax.all_to_all(jnp.broadcast_to(x[None], (n, per)), WIDE, 0, 0, tiled=True)  14.4 us
    all_to_all x1, blocking collectives, sum_all(): lax.all_to_all(jnp.broadcast_to(x[None], (m, per)), Z, 0, 0, tiled=True)  9.59 us
    reduce_sum x3, other arithmetic, col_lse(): totals = jnp.sum(jnp.exp(shifted - peaks[None, :]), axis=0)  5.44 us
    reduce_sum x3, other arithmetic, row_lse(): totals = jnp.sum(jnp.exp(shifted - peaks[:, None]), axis=1)  5.14 us

profile of v7, /device:TPU:1, one launch (start us, length us, event | category | flops | bytes accessed | tf_op | source)
XLA Modules:
  0.0 145.0 jit_solution(147778917026325292)
XLA Ops:
  0.6 0.0 copy-start
  0.6 2.5 %convolution_convert_fusion = bf16[300,1024]{1,0:T(8,128)(2,1)S(1)} fusion(f32[300,300]{1,0:T(8,128)} %param.7, bf16[300,1024]{1,0:T(8,128)(2,1)} %param.5), kind=kOutput, calls=%fused_computation.15 | convolution fusion | flops 1106227200 | bytes 1588800 | tf_op jit(solution)/shard_map/dot_general | solution.py:58
  3.2 2.5 %fusion.33 = (f32[1024]{0:T(1024)S(1)}, f32[1024,2048]{1,0:T(8,128)S(1)}) fusion(bf16[300,1024]{1,0:T(8,128)(2,1)S(1)} %convolution_convert_fusion, bf16[300,2048]{1,0:T(8,128)(2,1)S(1)} %copy-done), kind=kOutput, calls=%fused_computation.72 | convolution fusion | flops 1260387328 | bytes 10235904 | tf_op jit(solution)/shard_map/dot_general | solution.py:61
  5.7 1.3 exponential_reduce_fusion.5
  7.0 17.1 %all_to_all.51 = f32[16,2,1024]{2,1,0:T(2,128)S(1)} all-to-all(f32[16,2,1024]{2,1,0:T(2,128)S(1)} %broadcast_in_dim.16), channel_id=1, replica_groups=mesh['src'=16,'tzh'=4,'tzl'=2,'tc'=2] {'tc','tzh','tzl'}, dimensions={0} | all-to-all | bytes 262144 | tf_op jit(solution)/shard_map/all_to_all | solution.py:17
  24.2 0.1 fusion.32
  24.4 0.6 add_reduce_fusion.3
  25.0 1.8 %exponential_reduce_fusion.4 = f32[2048]{0:T(1024)S(1)} fusion(f32[1024,2048]{1,0:T(8,128)S(1)} %get-tuple-element.22, f32[2048]{0:T(1024)S(1)} %add_reduce_fusion.3, f32[1024]{0:T(1024)S(1)} %add_subtract_fusion.5), kind=kLoop, calls=%fused_computation.5 | loop fusion | flops 6289408 | bytes 8409088 | tf_op jit(solution)/shard_map/reduce_sum | solution.py:31
  26.9 0.1 broadcast_in_dim.17
  27.0 14.1 %all_to_all.52 = f32[16,2,2048]{2,1,0:T(2,128)S(1)} all-to-all(f32[16,2,2048]{2,1,0:T(2,128)S(1)} %broadcast_in_dim.17), channel_id=1, replica_groups=mesh['src'=16,'tzh'=4,'tzl'=2,'tc'=2] {'src'}, dimensions={0} | all-to-all | bytes 524288 | tf_op jit(solution)/shard_map/all_to_all | solution.py:17
  41.1 0.2 fusion.29
  41.3 0.1 fusion.14
  41.4 0.6 add_reduce_fusion.2
  42.0 1.9 %exponential_reduce_fusion.3 = f32[1024]{0:T(1024)S(1)} fusion(f32[1024,2048]{1,0:T(8,128)S(1)} %get-tuple-element.22, f32[1024]{0:T(1024)S(1)} %add_reduce_fusion.2, f32[2048]{0:T(1024)S(1)} %add_subtract_fusion.2), kind=kLoop, calls=%fused_computation.4 | loop fusion | flops 6290432 | bytes 8404992 | tf_op jit(solution)/shard_map/reduce_sum | solution.py:25
  44.0 13.0 %all_to_all.53 = f32[16,2,1024]{2,1,0:T(2,128)S(1)} all-to-all(f32[16,2,1024]{2,1,0:T(2,128)S(1)} %broadcast_in_dim.18), channel_id=1, replica_groups=mesh['src'=16,'tzh'=4,'tzl'=2,'tc'=2] {'tc','tzh','tzl'}, dimensions={0} | all-to-all | bytes 262144 | tf_op jit(solution)/shard_map/all_to_all | solution.py:17
  57.0 0.1 fusion.31
  57.2 0.6 add_reduce_fusion.1
  57.9 1.8 %exponential_reduce_fusion.2 = f32[2048]{0:T(1024)S(1)} fusion(f32[1024,2048]{1,0:T(8,128)S(1)} %get-tuple-element.22, f32[2048]{0:T(1024)S(1)} %add_reduce_fusion.1, f32[1024]{0:T(1024)S(1)} %add_subtract_fusion.4), kind=kLoop, calls=%fused_computation.3 | loop fusion | flops 6289408 | bytes 8409088 | tf_op jit(solution)/shard_map/reduce_sum | solution.py:31
  59.7 0.1 broadcast_in_dim.19
  59.8 10.2 %all_to_all.54 = f32[16,2,2048]{2,1,0:T(2,128)S(1)} all-to-all(f32[16,2,2048]{2,1,0:T(2,128)S(1)} %broadcast_in_dim.19), channel_id=1, replica_groups=mesh['src'=16,'tzh'=4,'tzl'=2,'tc'=2] {'src'}, dimensions={0} | all-to-all | bytes 524288 | tf_op jit(solution)/shard_map/all_to_all | solution.py:17
  70.0 0.2 fusion.28
  70.2 0.1 fusion.10
  70.3 0.6 add_reduce_fusion
  70.9 1.9 %exponential_reduce_fusion.1 = f32[1024]{0:T(1024)S(1)} fusion(f32[1024,2048]{1,0:T(8,128)S(1)} %get-tuple-element.22, f32[1024]{0:T(1024)S(1)} %add_reduce_fusion, f32[2048]{0:T(1024)S(1)} %add_subtract_fusion.1), kind=kLoop, calls=%fused_computation.2 | loop fusion | flops 6290432 | bytes 8404992 | tf_op jit(solution)/shard_map/reduce_sum | solution.py:25
  73.0 13.0 %all_to_all.55 = f32[16,2,1024]{2,1,0:T(2,128)S(1)} all-to-all(f32[16,2,1024]{2,1,0:T(2,128)S(1)} %broadcast_in_dim.20), channel_id=1, replica_groups=mesh['src'=16,'tzh'=4,'tzl'=2,'tc'=2] {'tc','tzh','tzl'}, dimensions={0} | all-to-all | bytes 262144 | tf_op jit(solution)/shard_map/all_to_all | solution.py:17
  85.9 0.1 fusion.30
  86.1 0.0 copy-start.3
  86.1 0.6 add_reduce_fusion.4
  86.8 1.8 %exponential_reduce_fusion = f32[2048]{0:T(1024)S(1)} fusion(f32[1024,2048]{1,0:T(8,128)S(1)} %get-tuple-element.22, f32[2048]{0:T(1024)S(1)} %add_reduce_fusion.4, f32[1024]{0:T(1024)S(1)} %add_subtract_fusion.3), kind=kLoop, calls=%fused_computation.1 | loop fusion | flops 6289408 | bytes 8409088 | tf_op jit(solution)/shard_map/reduce_sum | solution.py:31
  88.6 0.1 broadcast_in_dim.21
  88.7 10.2 %all_to_all.56 = f32[16,2,2048]{2,1,0:T(2,128)S(1)} all-to-all(f32[16,2,2048]{2,1,0:T(2,128)S(1)} %broadcast_in_dim.21), channel_id=1, replica_groups=mesh['src'=16,'tzh'=4,'tzl'=2,'tc'=2] {'src'}, dimensions={0} | all-to-all | bytes 524288 | tf_op jit(solution)/shard_map/all_to_all | solution.py:17
  98.9 0.2 fusion.27
  99.1 0.1 fusion.6
  99.3 0.0 copy-start.5
  99.3 1.7 %fusion = f32[1024,300]{0,1:T(8,128)S(1)} fusion(bf16[300,2048]{1,0:T(8,128)(2,1)S(1)} %copy-done, f32[1024,2048]{1,0:T(8,128)S(1)} %get-tuple-element.22, f32[2048]{0:T(1024)S(1)} %add_subtract_fusion, f32[1024]{0:T(1024)S(1)} %add_subtract_fusion.3), kind=kOutput, calls=%fused_computation.12 | convolution fusion | flops 1264582656 | bytes 10858496 | tf_op jit(solution)/shard_map/dot_general | solution.py:71
  101.0 1.1 convolution_bitcast_fusion
  102.1 0.2 copy.28
  102.3 0.5 reshape.59
  102.8 0.5 all_to_all.38
  103.3 14.8 %all_to_all.57 = f32[32,1,2813]{2,1,0:T(1,128)S(1)} all-to-all(f32[32,1,2813]{2,1,0:T(1,128)S(1)} %all_to_all.38), channel_id=1, replica_groups=mesh['src'=16,'tzh'=4,'tzl'=2,'tc'=2] {'tc','src'}, dimensions={0} | all-to-all | bytes 720128 | tf_op jit(solution)/shard_map/all_to_all | solution.py:51
  118.1 0.2 reduce_sum.138
  118.4 9.6 %all_to_all.58 = f32[8,1,2813]{2,1,0:T(1,128)S(1)} all-to-all(f32[8,1,2813]{2,1,0:T(1,128)S(1)} %broadcast_in_dim.22), channel_id=1, replica_groups=mesh['src'=16,'tzh'=4,'tzl'=2,'tc'=2] {'tzl','tzh'}, dimensions={0} | all-to-all | bytes 180032 | tf_op jit(solution)/shard_map/all_to_all | solution.py:52
  128.0 0.1 reduce_sum.139
  128.0 0.2 broadcast_in_dim.23
  128.2 14.4 %all_to_all.59 = f32[32,1,2813]{2,1,0:T(1,128)S(1)} all-to-all(f32[32,1,2813]{2,1,0:T(1,128)S(1)} %broadcast_in_dim.23), channel_id=1, replica_groups=mesh['src'=16,'tzh'=4,'tzl'=2,'tc'=2] {'tc','src'}, dimensions={0} | all-to-all | bytes 720128 | tf_op jit(solution)/shard_map/all_to_all | solution.py:53
  142.7 0.8 reduce.8
  143.5 0.2 reshape.60
  143.8 1.2 reshape.61
  (30 shorter events, 0.5 us)
Async XLA Ops:
  0.6 2.5 %copy-start = (bf16[300,2048]{1,0:T(8,128)(2,1)S(1)}, bf16[300,2048]{1,0:T(8,128)(2,1)}, u32[]{:S(2)}) copy-start(bf16[300,2048]{1,0:T(8,128)(2,1)} %param.6) | copy-start | bytes 3686404
  3.2 21.2 %copy-start.4 = (f32[1024]{0:T(1024)S(1)}, f32[1024]{0:T(1024)}, u32[]{:S(2)}) copy-start(f32[1024]{0:T(1024)} %param.8) | copy-start | bytes 12292
  24.4 17.0 %copy-start.2 = (f32[2048]{0:T(1024)S(1)}, f32[2048]{0:T(1024)}, u32[]{:S(2)}) copy-start(f32[2048]{0:T(1024)} %param.9) | copy-start | bytes 24580
  86.1 13.1 %copy-start.3 = (f32[1024]{0:T(1024)}, f32[1024]{0:T(1024)S(1)}, u32[]{:S(2)}) copy-start(f32[1024]{0:T(1024)S(1)} %add_subtract_fusion.3) | copy-start | bytes 12292
  99.3 1.7 %copy-start.5 = (f32[2048]{0:T(1024)}, f32[2048]{0:T(1024)S(1)}, u32[]{:S(2)}) copy-start(f32[2048]{0:T(1024)S(1)} %add_subtract_fusion) | copy-start | bytes 24580
  99.3 1.7 %copy-start.1 = (bf16[300,1024]{1,0:T(8,128)(2,1)S(1)}, bf16[300,1024]{1,0:T(8,128)(2,1)}, u32[]{:S(2)}) copy-start(bf16[300,1024]{1,0:T(8,128)(2,1)} %param.5) | copy-start | bytes 1843204

commit v8 on v7

--- a/solution.py
+++ b/solution.py
@@ -10,26 +10,32 @@
 WIDE = ("tc", "src")
 
 
-def merge_lse(peaks, totals, axis):
-    n = lax.axis_size(axis)
-    pair = jnp.stack([peaks, totals])
-    sent = jnp.broadcast_to(pair[None], (n,) + pair.shape)
-    got = lax.all_to_all(sent, axis, 0, 0, tiled=False)
-    top = jnp.max(got[:, 0], axis=0)
-    total = jnp.sum(got[:, 1] * jnp.exp(got[:, 0] - top[None]), axis=0)
-    return top + jnp.log(total)
+def merge_lse(peaks, totals, axes):
+    for axis in axes:
+        n = lax.axis_size(axis)
+        pair = jnp.stack([peaks, totals])
+        if n == 2:
+            other = lax.ppermute(pair, axis, [(0, 1), (1, 0)])
+            top = jnp.maximum(peaks, other[0])
+            totals = totals * jnp.exp(peaks - top) + other[1] * jnp.exp(other[0] - top)
+            peaks = top
+        else:
+            got = lax.all_to_all(jnp.broadcast_to(pair[None], (n,) + pair.shape), axis, 0, 0, tiled=False)
+            peaks = jnp.max(got[:, 0], axis=0)
+            totals = jnp.sum(got[:, 1] * jnp.exp(got[:, 0] - peaks[None]), axis=0)
+    return peaks + jnp.log(totals)
 
 
 def row_lse(shifted):
     peaks = jnp.max(shifted, axis=1)
     totals = jnp.sum(jnp.exp(shifted - peaks[:, None]), axis=1)
-    return merge_lse(peaks, totals, ("tc", "tzh", "tzl"))
+    return merge_lse(peaks, totals, ("tc", ("tzl", "tzh")))
 
 
 def col_lse(shifted):
     peaks = jnp.max(shifted, axis=0)
     totals = jnp.sum(jnp.exp(shifted - peaks[None, :]), axis=0)
-    return merge_lse(peaks, totals, "src")
+    return merge_lse(peaks, totals, ("src",))
 
 
 def butterfly_sum(x, axis):

time: 145 us -> 145 us (level)
  blocking collectives: 116 us -> 104 us
  starting transfers between devices: 0 us -> 9.37 us
  waiting for transfers between devices: 0 us -> 2.49 us
    all_to_all x6, blocking collectives: 77.6 us -> 65.7 us  [merge_lse(): lax.all_to_all(jnp.broadcast_to(pair[None], (n,) + pair.shape), axis, 0,...]
    ppermute x0 -> x3, starting transfers between devices: none -> 9.37 us  [merge_lse(): other = lax.ppermute(pair, axis, [(0, 1), (1, 0)])]
    ppermute x0 -> x3, waiting for transfers between devices: none -> 2.49 us  [merge_lse(): other = lax.ppermute(pair, axis, [(0, 1), (1, 0)])]
  transfers between devices with their start and end apart: 0 -> 3, of which waited for: 0 -> 3; matrix products, arithmetic and copies ran while one was open for 0% -> 0% of each run, Pallas kernels for 0% -> 0%
where the time goes in v8:
time: 145 us
  blocking collectives  104 us (72%)
  other arithmetic  16.4 us (11%)
  starting transfers between devices  9.37 us (6%)
  matrix products  7.83 us (5%)
  local copies, waits for them, and re-layouts  3.24 us (2%)
  waiting for transfers between devices  2.49 us (2%)
    all_to_all x6, blocking collectives, merge_lse(): lax.all_to_all(jnp.broadcast_to(pair[None], (n,) + pair.shape), axis, 0,...  65.7 us
    all_to_all x1, blocking collectives, sum_all(): x = jnp.sum(lax.all_to_all(x, WIDE, 0, 0, tiled=True), axis=0)  14.8 us
    all_to_all x1, blocking collectives, sum_all(): lax.all_to_all(jnp.broadcast_to(x[None], (n, per)), WIDE, 0, 0, tiled=True)  14.4 us
    ppermute x3, starting transfers between devices, merge_lse(): other = lax.ppermute(pair, axis, [(0, 1), (1, 0)])  9.37 us
    all_to_all x1, blocking collectives, sum_all(): lax.all_to_all(jnp.broadcast_to(x[None], (m, per)), Z, 0, 0, tiled=True)  9.25 us
    reduce_sum x3, other arithmetic, col_lse(): totals = jnp.sum(jnp.exp(shifted - peaks[None, :]), axis=0)  5.44 us
    reduce_sum x3, other arithmetic, row_lse(): totals = jnp.sum(jnp.exp(shifted - peaks[:, None]), axis=1)  5.14 us
  transfers between devices with their start and end apart: 3, of which 3 were waited for; matrix products, arithmetic and copies ran while one was open for 0% of the time, Pallas kernels for 0%

profile of v8, /device:TPU:1, one launch (start us, length us, event | category | flops | bytes accessed | tf_op | source)
XLA Modules:
  0.0 144.5 jit_solution(2826314509660516027)
XLA Ops:
  0.6 2.5 %convolution_convert_fusion = bf16[300,1024]{1,0:T(8,128)(2,1)S(1)} fusion(f32[300,300]{1,0:T(8,128)} %param.7, bf16[300,1024]{1,0:T(8,128)(2,1)} %param.5), kind=kOutput, calls=%fused_computation.15 | convolution fusion | flops 1106227200 | bytes 1588800 | tf_op jit(solution)/shard_map/dot_general | solution.py:64
  3.2 2.5 %fusion.36 = (f32[1024]{0:T(1024)S(1)}, f32[1024,2048]{1,0:T(8,128)S(1)}) fusion(bf16[300,1024]{1,0:T(8,128)(2,1)S(1)} %convolution_convert_fusion, bf16[300,2048]{1,0:T(8,128)(2,1)S(1)} %copy-done), kind=kOutput, calls=%fused_computation.84 | convolution fusion | flops 1260387328 | bytes 10235904 | tf_op jit(solution)/shard_map/dot_general | solution.py:67
  5.7 1.3 exponential_reduce_fusion.5
  7.0 3.3 %collective-permute-start = (f32[2,1024]{1,0:T(2,128)S(1)}, f32[2,1024]{1,0:T(2,128)S(1)}, u32[]{:S(2)}, u32[]{:S(2)}) collective-permute-start(f32[2,1024]{1,0:T(2,128)S(1)} %pad_maximum_fusion.3), channel_id=1, source_target_pairs={{0,1},{1,0},{2,3},{3,2},{4,5},{5,4},{6,7},{7,6},{8,9},{9,8},{10,11... | collective-permute-start | bytes 24584 | tf_op jit(solution)/shard_map/ppermute | solution.py:18
  10.3 0.8 collective-permute-done
  11.2 12.9 %all_to_all.51 = f32[8,2,1024]{2,1,0:T(2,128)S(1)} all-to-all(f32[8,2,1024]{2,1,0:T(2,128)S(1)} %broadcast_in_dim.16), channel_id=1, replica_groups=mesh['src'=16,'tzh'=4,'tzl'=2,'tc'=2] {'tzl','tzh'}, dimensions={0} | all-to-all | bytes 131072 | tf_op jit(solution)/shard_map/all_to_all | solution.py:23
  24.2 0.6 add_reduce_fusion.3
  24.8 1.8 %exponential_reduce_fusion.4 = f32[2048]{0:T(1024)S(1)} fusion(f32[1024,2048]{1,0:T(8,128)S(1)} %get-tuple-element.28, f32[2048]{0:T(1024)S(1)} %add_reduce_fusion.3, f32[1024]{0:T(1024)S(1)} %add_subtract_fusion.5), kind=kLoop, calls=%fused_computation.5 | loop fusion | flops 6289408 | bytes 8409088 | tf_op jit(solution)/shard_map/reduce_sum | solution.py:37
  26.7 0.1 broadcast_in_dim.17
  26.8 14.1 %all_to_all.52 = f32[16,2,2048]{2,1,0:T(2,128)S(1)} all-to-all(f32[16,2,2048]{2,1,0:T(2,128)S(1)} %broadcast_in_dim.17), channel_id=1, replica_groups=mesh['src'=16,'tzh'=4,'tzl'=2,'tc'=2] {'src'}, dimensions={0} | all-to-all | bytes 524288 | tf_op jit(solution)/shard_map/all_to_all | solution.py:23
  40.9 0.2 fusion.32
  41.1 0.1 fusion.14
  41.3 0.6 add_reduce_fusion.2
  41.9 1.9 %exponential_reduce_fusion.3 = f32[1024]{0:T(1024)S(1)} fusion(f32[1024,2048]{1,0:T(8,128)S(1)} %get-tuple-element.28, f32[1024]{0:T(1024)S(1)} %add_reduce_fusion.2, f32[2048]{0:T(1024)S(1)} %add_subtract_fusion.2), kind=kLoop, calls=%fused_computation.4 | loop fusion | flops 6290432 | bytes 8404992 | tf_op jit(solution)/shard_map/reduce_sum | solution.py:31
  43.8 3.3 %collective-permute-start.1 = (f32[2,1024]{1,0:T(2,128)S(1)}, f32[2,1024]{1,0:T(2,128)S(1)}, u32[]{:S(2)}, u32[]{:S(2)}) collective-permute-start(f32[2,1024]{1,0:T(2,128)S(1)} %pad_maximum_fusion.5), channel_id=1, source_target_pairs={{0,1},{1,0},{2,3},{3,2},{4,5},{5,4},{6,7},{7,6},{8,9},{9,8},{10,11... | collective-permute-start | bytes 24584 | tf_op jit(solution)/shard_map/ppermute | solution.py:18
  47.1 0.8 collective-permute-done.1
  48.0 9.1 %all_to_all.53 = f32[8,2,1024]{2,1,0:T(2,128)S(1)} all-to-all(f32[8,2,1024]{2,1,0:T(2,128)S(1)} %broadcast_in_dim.18), channel_id=1, replica_groups=mesh['src'=16,'tzh'=4,'tzl'=2,'tc'=2] {'tzl','tzh'}, dimensions={0} | all-to-all | bytes 131072 | tf_op jit(solution)/shard_map/all_to_all | solution.py:23
  57.2 0.6 add_reduce_fusion.1
  57.9 1.8 %exponential_reduce_fusion.2 = f32[2048]{0:T(1024)S(1)} fusion(f32[1024,2048]{1,0:T(8,128)S(1)} %get-tuple-element.28, f32[2048]{0:T(1024)S(1)} %add_reduce_fusion.1, f32[1024]{0:T(1024)S(1)} %add_subtract_fusion.4), kind=kLoop, calls=%fused_computation.3 | loop fusion | flops 6289408 | bytes 8409088 | tf_op jit(solution)/shard_map/reduce_sum | solution.py:37
  59.7 0.1 broadcast_in_dim.19
  59.8 10.3 %all_to_all.54 = f32[16,2,2048]{2,1,0:T(2,128)S(1)} all-to-all(f32[16,2,2048]{2,1,0:T(2,128)S(1)} %broadcast_in_dim.19), channel_id=1, replica_groups=mesh['src'=16,'tzh'=4,'tzl'=2,'tc'=2] {'src'}, dimensions={0} | all-to-all | bytes 524288 | tf_op jit(solution)/shard_map/all_to_all | solution.py:23
  70.1 0.2 fusion.31
  70.3 0.1 fusion.10
  70.4 0.6 add_reduce_fusion
  71.0 1.9 %exponential_reduce_fusion.1 = f32[1024]{0:T(1024)S(1)} fusion(f32[1024,2048]{1,0:T(8,128)S(1)} %get-tuple-element.28, f32[1024]{0:T(1024)S(1)} %add_reduce_fusion, f32[2048]{0:T(1024)S(1)} %add_subtract_fusion.1), kind=kLoop, calls=%fused_computation.2 | loop fusion | flops 6290432 | bytes 8404992 | tf_op jit(solution)/shard_map/reduce_sum | solution.py:31
  73.0 2.8 %collective-permute-start.2 = (f32[2,1024]{1,0:T(2,128)S(1)}, f32[2,1024]{1,0:T(2,128)S(1)}, u32[]{:S(2)}, u32[]{:S(2)}) collective-permute-start(f32[2,1024]{1,0:T(2,128)S(1)} %pad_maximum_fusion.7), channel_id=1, source_target_pairs={{0,1},{1,0},{2,3},{3,2},{4,5},{5,4},{6,7},{7,6},{8,9},{9,8},{10,11... | collective-permute-start | bytes 24584 | tf_op jit(solution)/shard_map/ppermute | solution.py:18
  75.8 0.8 collective-permute-done.2
  76.7 9.2 %all_to_all.55 = f32[8,2,1024]{2,1,0:T(2,128)S(1)} all-to-all(f32[8,2,1024]{2,1,0:T(2,128)S(1)} %broadcast_in_dim.20), channel_id=1, replica_groups=mesh['src'=16,'tzh'=4,'tzl'=2,'tc'=2] {'tzl','tzh'}, dimensions={0} | all-to-all | bytes 131072 | tf_op jit(solution)/shard_map/all_to_all | solution.py:23
  86.0 0.6 add_reduce_fusion.4
  86.7 1.8 %exponential_reduce_fusion = f32[2048]{0:T(1024)S(1)} fusion(f32[1024,2048]{1,0:T(8,128)S(1)} %get-tuple-element.28, f32[2048]{0:T(1024)S(1)} %add_reduce_fusion.4, f32[1024]{0:T(1024)S(1)} %add_subtract_fusion.3), kind=kLoop, calls=%fused_computation.1 | loop fusion | flops 6289408 | bytes 8409088 | tf_op jit(solution)/shard_map/reduce_sum | solution.py:37
  88.5 0.1 broadcast_in_dim.21
  88.6 10.2 %all_to_all.56 = f32[16,2,2048]{2,1,0:T(2,128)S(1)} all-to-all(f32[16,2,2048]{2,1,0:T(2,128)S(1)} %broadcast_in_dim.21), channel_id=1, replica_groups=mesh['src'=16,'tzh'=4,'tzl'=2,'tc'=2] {'src'}, dimensions={0} | all-to-all | bytes 524288 | tf_op jit(solution)/shard_map/all_to_all | solution.py:23
  98.8 0.2 fusion.30
  99.0 0.1 fusion.6
  99.2 1.7 %fusion = f32[1024,300]{0,1:T(8,128)S(1)} fusion(bf16[300,2048]{1,0:T(8,128)(2,1)S(1)} %copy-done, f32[1024,2048]{1,0:T(8,128)S(1)} %get-tuple-element.28, f32[2048]{0:T(1024)S(1)} %add_subtract_fusion, f32[1024]{0:T(1024)S(1)} %add_subtract_fusion.3), kind=kOutput, calls=%fused_computation.12 | convolution fusion | flops 1264582656 | bytes 10858496 | tf_op jit(solution)/shard_map/dot_general | solution.py:77
  100.9 1.1 convolution_bitcast_fusion
  102.0 0.2 copy.28
  102.2 0.5 reshape.68
  102.7 0.5 all_to_all.38
  103.2 14.8 %all_to_all.57 = f32[32,1,2813]{2,1,0:T(1,128)S(1)} all-to-all(f32[32,1,2813]{2,1,0:T(1,128)S(1)} %all_to_all.38), channel_id=1, replica_groups=mesh['src'=16,'tzh'=4,'tzl'=2,'tc'=2] {'tc','src'}, dimensions={0} | all-to-all | bytes 720128 | tf_op jit(solution)/shard_map/all_to_all | solution.py:57
  118.0 0.2 reduce_sum.138
  118.3 9.2 %all_to_all.58 = f32[8,1,2813]{2,1,0:T(1,128)S(1)} all-to-all(f32[8,1,2813]{2,1,0:T(1,128)S(1)} %broadcast_in_dim.22), channel_id=1, replica_groups=mesh['src'=16,'tzh'=4,'tzl'=2,'tc'=2] {'tzl','tzh'}, dimensions={0} | all-to-all | bytes 180032 | tf_op jit(solution)/shard_map/all_to_all | solution.py:58
  127.5 0.1 reduce_sum.139
  127.6 0.2 broadcast_in_dim.23
  127.8 14.4 %all_to_all.59 = f32[32,1,2813]{2,1,0:T(1,128)S(1)} all-to-all(f32[32,1,2813]{2,1,0:T(1,128)S(1)} %broadcast_in_dim.23), channel_id=1, replica_groups=mesh['src'=16,'tzh'=4,'tzl'=2,'tc'=2] {'tc','src'}, dimensions={0} | all-to-all | bytes 720128 | tf_op jit(solution)/shard_map/all_to_all | solution.py:59
  142.2 0.8 reduce.8
  143.1 0.2 reshape.69
  143.3 1.2 reshape.70
  (42 shorter events, 0.7 us)
Async XLA Ops:
  0.6 2.5 %copy-start = (bf16[300,2048]{1,0:T(8,128)(2,1)S(1)}, bf16[300,2048]{1,0:T(8,128)(2,1)}, u32[]{:S(2)}) copy-start(bf16[300,2048]{1,0:T(8,128)(2,1)} %param.6) | copy-start | bytes 3686404
  3.2 21.0 %copy-start.4 = (f32[1024]{0:T(1024)S(1)}, f32[1024]{0:T(1024)}, u32[]{:S(2)}) copy-start(f32[1024]{0:T(1024)} %param.8) | copy-start | bytes 12292
  7.0 4.1 %collective-permute-start = (f32[2,1024]{1,0:T(2,128)S(1)}, f32[2,1024]{1,0:T(2,128)S(1)}, u32[]{:S(2)}, u32[]{:S(2)}) collective-permute-start(f32[2,1024]{1,0:T(2,128)S(1)} %pad_maximum_fusion.3), channel_id=1, source_target_pairs={{0,1},{1,0},{2,3},{3,2},{4,5},{5,4},{6,7},{7,6},{8,9},{9,8},{10,11... | collective-permute-start | bytes 24584 | tf_op jit(solution)/shard_map/ppermute | solution.py:18
  24.2 17.0 %copy-start.2 = (f32[2048]{0:T(1024)S(1)}, f32[2048]{0:T(1024)}, u32[]{:S(2)}) copy-start(f32[2048]{0:T(1024)} %param.9) | copy-start | bytes 24580
  43.8 4.1 %collective-permute-start.1 = (f32[2,1024]{1,0:T(2,128)S(1)}, f32[2,1024]{1,0:T(2,128)S(1)}, u32[]{:S(2)}, u32[]{:S(2)}) collective-permute-start(f32[2,1024]{1,0:T(2,128)S(1)} %pad_maximum_fusion.5), channel_id=1, source_target_pairs={{0,1},{1,0},{2,3},{3,2},{4,5},{5,4},{6,7},{7,6},{8,9},{9,8},{10,11... | collective-permute-start | bytes 24584 | tf_op jit(solution)/shard_map/ppermute | solution.py:18
  73.0 3.6 %collective-permute-start.2 = (f32[2,1024]{1,0:T(2,128)S(1)}, f32[2,1024]{1,0:T(2,128)S(1)}, u32[]{:S(2)}, u32[]{:S(2)}) collective-permute-start(f32[2,1024]{1,0:T(2,128)S(1)} %pad_maximum_fusion.7), channel_id=1, source_target_pairs={{0,1},{1,0},{2,3},{3,2},{4,5},{5,4},{6,7},{7,6},{8,9},{9,8},{10,11... | collective-permute-start | bytes 24584 | tf_op jit(solution)/shard_map/ppermute | solution.py:18
  86.0 13.1 %copy-start.3 = (f32[1024]{0:T(1024)}, f32[1024]{0:T(1024)S(1)}, u32[]{:S(2)}) copy-start(f32[1024]{0:T(1024)S(1)} %add_subtract_fusion.3) | copy-start | bytes 12292
  99.1 1.7 %copy-start.5 = (f32[2048]{0:T(1024)}, f32[2048]{0:T(1024)S(1)}, u32[]{:S(2)}) copy-start(f32[2048]{0:T(1024)S(1)} %add_subtract_fusion) | copy-start | bytes 24580
  99.2 1.7 %copy-start.1 = (bf16[300,1024]{1,0:T(8,128)(2,1)S(1)}, bf16[300,1024]{1,0:T(8,128)(2,1)}, u32[]{:S(2)}) copy-start(bf16[300,1024]{1,0:T(8,128)(2,1)} %param.5) | copy-start | bytes 1843204
